TPU v7x, 128 devices: a whole 4x4x4 slice. The times are simulated.
128 devices in a mesh: expert: 32 (over y, z, core), ffn: 4 (over x).
Axes of the slice: x: 4, y: 4, z: 4, core: 2. Of those that a mesh axis runs over, the one named last changes fastest.
Arguments:
- tokens: bfloat16 [16384, 768], P('expert', 'ffn'), may hold values from -6 to 6
- cotangent: bfloat16 [16384, 768], P('expert', 'ffn'), may hold values from -6 to 6
- gates: float32 [16384, 2], P('expert'), may hold values from 0.2 to 1
- expert_ids: int32 [16384, 2], P('expert'), may hold values from 0 to 63, all different within a row; in each aligned block of 512 rows (0 to 511, 512 to 1023, ...) at most 32 rows name the same one
- up_weight: bfloat16 [64, 768, 3072], P('expert', None, 'ffn'), may hold values from -0.21875 to 0.21875
- down_weight: bfloat16 [64, 3072, 768], P('expert', 'ffn'), may hold values from -0.109375 to 0.109375
Outputs:
- layer_out: bfloat16 [16384, 768], P('expert', 'ffn')
- grad_tokens: bfloat16 [16384, 768], P('expert', 'ffn')
- grad_up: bfloat16 [64, 768, 3072], P('expert', None, 'ffn')
- grad_down: bfloat16 [64, 3072, 768], P('expert', 'ffn')
Inputs may be any that keep to these rules, and one draw needn't show every extreme that they name: `expert_ids`: the two experts of a token differ. Among the tokens of one index of expert no expert is named more than 32 times, a bound that some block reaches.
All inputs are finite; a program needn't handle non-finite values.
Results may differ from a plain program's by a relative error of at most 0.0065.
Values may be sent and summed in bfloat16 or wider, within the bound.
No kernel may reach another device: no remote copies, remote signals or barrier semaphores. Data moves between devices by JAX's collectives and lax.ppermute only.
A program may use at most 192 MiB of HBM per device.

v0:
```python
import jax
import jax.numpy as jnp
from jax import lax
from jax.experimental.layout import Layout, with_layout_constraint
from jax.sharding import PartitionSpec as P


def slot_targets(expert_ids, owners, local_experts, capacity):
    flat_ids = expert_ids.reshape(-1)
    count = flat_ids.shape[0]
    experts = owners * local_experts
    columns = lax.broadcasted_iota(jnp.int32, (count, experts), 1)
    onehot = (flat_ids[:, None] == columns).astype(jnp.bfloat16)
    earlier = (
        lax.broadcasted_iota(jnp.int32, (count, count), 0)
        > lax.broadcasted_iota(jnp.int32, (count, count), 1)
    ).astype(jnp.bfloat16)
    before = jnp.dot(earlier, onehot, preferred_element_type=jnp.float32)
    position = jnp.sum(onehot.astype(jnp.float32) * before, axis=1).astype(jnp.int32)
    return (flat_ids % local_experts) * (owners * capacity) + (flat_ids // local_experts) * capacity + position


def shards(tokens, cotangent, gates, expert_ids, up_weight, down_weight):
    owners = lax.axis_size("expert")
    local_experts = up_weight.shape[0]
    experts = owners * local_experts
    tok_rows = tokens.shape[0]
    capacity = 2 * tok_rows // owners
    rows = experts * capacity
    slots = owners * capacity
    target = slot_targets(expert_ids, owners, local_experts, capacity)
    row_ids = lax.broadcasted_iota(jnp.int32, (rows, 2 * tok_rows), 0)
    placer = (row_ids == target[None, :]).astype(jnp.bfloat16)
    tok_ids = lax.broadcasted_iota(jnp.int32, (rows, tok_rows), 0)
    pair = target.reshape(tok_rows, 2)
    token_placer = ((tok_ids == pair[None, :, 0]) | (tok_ids == pair[None, :, 1])).astype(
        jnp.bfloat16
    )
    weights = gates.reshape(-1)

    whole_tokens = lax.all_gather(tokens, "ffn", axis=1, tiled=True)
    whole_cot = lax.all_gather(cotangent, "ffn", axis=1, tiled=True)

    def dispatch(send):
        send = send.astype(jnp.bfloat16).reshape(local_experts, owners, capacity, send.shape[1])
        got = lax.all_to_all(send, "expert", split_axis=1, concat_axis=1, tiled=True)
        return got.reshape(local_experts, slots, got.shape[3])

    rows_in = dispatch(jnp.dot(token_placer, whole_tokens, preferred_element_type=jnp.float32))
    assigned = (weights[:, None] * jnp.repeat(whole_cot, 2, axis=0).astype(jnp.float32)).astype(
        jnp.bfloat16
    )
    grads_in = dispatch(jnp.dot(placer, assigned, preferred_element_type=jnp.float32))

    def send_home(parts):
        cols = jnp.stack(
            [
                lax.psum_scatter(
                    with_layout_constraint(part, Layout((0, 1))),
                    "ffn",
                    scatter_dimension=0,
                    tiled=True,
                )
                for part in parts
            ],
            axis=1,
        ).astype(jnp.bfloat16)
        cols = cols.reshape(cols.shape[0], local_experts, owners, capacity)
        back = lax.all_to_all(cols, "expert", split_axis=2, concat_axis=2, tiled=True)
        return back.reshape(back.shape[0], rows)

    preact = jnp.einsum("xsd,xdf->xsf", rows_in, up_weight, preferred_element_type=jnp.float32)
    gating = jax.nn.sigmoid(preact)
    activated = (preact * gating).astype(jnp.bfloat16)
    out_part = [
        jnp.einsum("fd,sf->ds", down_weight[x], activated[x], preferred_element_type=jnp.float32)
        for x in range(local_experts)
    ]
    out_home = send_home(out_part)
    back_grad = jnp.einsum(
        "xsd,xfd->xsf", grads_in, down_weight, preferred_element_type=jnp.float32
    )
    pre_grad = (back_grad * gating * (1.0 + preact * (1.0 - gating))).astype(jnp.bfloat16)
    grad_down = jnp.einsum(
        "xsf,xsd->xfd", activated, grads_in, preferred_element_type=jnp.float32
    ).astype(jnp.bfloat16)
    grad_up = jnp.einsum(
        "xsd,xsf->xdf", rows_in, pre_grad, preferred_element_type=jnp.float32
    ).astype(jnp.bfloat16)
    in_part = [
        jnp.einsum("df,sf->ds", up_weight[x], pre_grad[x], preferred_element_type=jnp.float32)
        for x in range(local_experts)
    ]
    in_home = send_home(in_part)

    def gather_back(returned):
        picked = lax.dot_general(
            placer, returned, (((0,), (1,)), ((), ())), preferred_element_type=jnp.float32
        )
        return picked.reshape(tok_rows, 2, returned.shape[0])

    layer_out = jnp.sum(gates[:, :, None] * gather_back(out_home), axis=1).astype(jnp.bfloat16)
    grad_tokens = jnp.sum(gather_back(in_home), axis=1).astype(jnp.bfloat16)
    return (layer_out, grad_tokens, grad_up, grad_down)


def solution(mesh):
    placed = (
        P("expert", "ffn"),
        P("expert", "ffn"),
        P("expert", None),
        P("expert", None),
        P("expert", None, "ffn"),
        P("expert", "ffn", None),
    )
    return jax.shard_map(
        shards,
        mesh=mesh,
        in_specs=placed,
        out_specs=(
            P("expert", "ffn"),
            P("expert", "ffn"),
            P("expert", None, "ffn"),
            P("expert", "ffn", None),
        ),
        check_vma=False,
    )
```

profile of v0, /device:TPU:1, one launch (start us, length us, event | category | flops | bytes accessed | tf_op | source)
XLA Modules:
  0.0 334.7 jit_solution(1738526114482320215)
XLA Ops:
  10.5 12.9 %all_gather.6 = bf16[512,768]{0,1:T(8,128)(2,1)S(1)} all-gather(bf16[512,192]{0,1:T(8,128)(2,1)S(1)} %copy-done.3), channel_id=1, replica_groups=mesh['expert'=32,'ffn'=4] {'ffn'}, dimensions={1}, use_global_device_ids=true | all-gather | bytes 983040 | tf_op jit(solution)/shard_map/all_gather | solution.py:41
  27.4 10.5 %all-to-all-start = ((bf16[2,32,32,768]{3,2,0,1:T(8,128)(2,1)}), bf16[2,32,32,768]{3,2,0,1:T(8,128)(2,1)S(1)}, u32[]{:S(2)}, u32[]{:S(2)}) async-start(bf16[2,32,32,768]{3,2,0,1:T(8,128)(2,1)} %copy.63), calls=%async_computation | async-start | bytes 6291456 | tf_op jit(solution)/shard_map/all_to_all | solution.py:46
  37.9 13.0 %all_gather.7 = bf16[512,768]{0,1:T(8,128)(2,1)} all-gather(bf16[512,192]{0,1:T(8,128)(2,1)S(1)} %copy-done.4), channel_id=1, replica_groups=mesh['expert'=32,'ffn'=4] {'ffn'}, dimensions={1}, use_global_device_ids=true | all-gather | bytes 983040 | tf_op jit(solution)/shard_map/all_gather | solution.py:42
  57.6 5.4 %convert_element_type.66 = f32[1024,768]{1,0:T(8,128)} reshape(f32[512,2,768]{2,1,0:T(2,128)} %broadcast_in_dim.2) | data formatting | bytes 6291456 | tf_op jit(solution)/shard_map/convert_element_type | solution.py:50
  63.3 6.0 %fusion.9 = bf16[2048,768]{1,0:T(8,128)(2,1)S(1)} fusion(s32[1024]{0:T(1024)S(1)} %fusion.48, f32[1024,768]{1,0:T(8,128)} %convert_element_type.66, f32[1024]{0:T(1024)S(1)} %mul.75), kind=kOutput, calls=%fused_computation.14 | convolution fusion | flops 3226468352 | bytes 6299648 | tf_op jit(solution)/shard_map/dot_general | solution.py:53
  71.4 6.3 %all-to-all-done = bf16[2,32,32,768]{3,2,0,1:T(8,128)(2,1)S(1)} async-done(((bf16[2,32,32,768]{3,2,0,1:T(8,128)(2,1)}), bf16[2,32,32,768]{3,2,0,1:T(8,128)(2,1)S(1)}, u32[]{:S(2)}, u32[]{:S(2)}) %all-to-all-start) | async-done | bytes 3145760 | tf_op jit(solution)/shard_map/all_to_all | solution.py:46
  77.7 5.1 %all-to-all-start.2 = ((bf16[2,32,32,768]{3,2,0,1:T(8,128)(2,1)}), bf16[2,32,32,768]{3,2,0,1:T(8,128)(2,1)}, u32[]{:S(2)}, u32[]{:S(2)}) async-start(bf16[2,32,32,768]{3,2,0,1:T(8,128)(2,1)} %copy.73), calls=%async_computation.4 | async-start | bytes 6291456 | tf_op jit(solution)/shard_map/all_to_all | solution.py:46
  85.7 5.4 %multiply_convert_fusion.1 = (bf16[2,1024,768]{2,1,0:T(8,128)(2,1)}, f32[2,1024,768]{2,1,0:T(8,128)}) fusion(bf16[2,1024,768]{2,1,0:T(8,128)(2,1)S(1)} %bitcast.59, bf16[2,768,768]{2,1,0:T(8,128)(2,1)S(1)} %copy-done.6), kind=kOutput, calls=%fused_computation.4 | convolution fusion | flops 2423783424 | bytes 14942208 | tf_op jit(solution)/shard_map/xsd,xdf->xsf/dot_general | solution.py:72
  91.1 31.5 %all-to-all-done.2 = bf16[2,32,32,768]{3,2,0,1:T(8,128)(2,1)} async-done(((bf16[2,32,32,768]{3,2,0,1:T(8,128)(2,1)}), bf16[2,32,32,768]{3,2,0,1:T(8,128)(2,1)}, u32[]{:S(2)}, u32[]{:S(2)}) %all-to-all-start.2) | async-done | bytes 3145760 | tf_op jit(solution)/shard_map/all_to_all | solution.py:46
  125.3 6.6 %multiply_convert_fusion = bf16[2,1024,768]{2,1,0:T(8,128)(2,1)S(1)} fusion(f32[2,1024,768]{2,1,0:T(8,128)} %get-tuple-element.7, bf16[2,1024,768]{2,1,0:T(8,128)(2,1)S(1)} %bitcast.57, bf16[2,768,768]{2,1,0:T(8,128)(2,1)S(1)} %copy-done.8), kind=kOutput, calls=%fused_computation.3 | convolution fusion | flops 2430074880 | bytes 14942208 | tf_op jit(solution)/shard_map/xsd,xfd->xsf/dot_general | solution.py:80
  136.7 4.6 %convolution_bitcast_fusion = f32[768,1024]{1,0:T(8,128)} fusion(bf16[2,1024,768]{2,1,0:T(8,128)(2,1)} %copy-done.10, bf16[2,768,768]{2,1,0:T(8,128)(2,1)S(1)} %copy-done.7), kind=kOutput, calls=%fused_computation.24 | convolution fusion | flops 1207959552 | bytes 5898240 | tf_op jit(solution)/shard_map/df,sf->ds/dot_general | solution.py:91
  143.0 4.9 %convolution_bitcast_fusion.3 = f32[768,1024]{1,0:T(8,128)} fusion(bf16[2,1024,768]{2,1,0:T(8,128)(2,1)} %get-tuple-element.6, bf16[2,768,768]{2,1,0:T(8,128)(2,1)S(1)} %copy-done.9), kind=kOutput, calls=%fused_computation.27 | convolution fusion | flops 1207959552 | bytes 5898240 | tf_op jit(solution)/shard_map/fd,sf->ds/dot_general | solution.py:76
  148.0 4.5 %convolution_bitcast_fusion.2 = f32[768,1024]{1,0:T(8,128)} fusion(bf16[2,1024,768]{2,1,0:T(8,128)(2,1)} %get-tuple-element.6, bf16[2,768,768]{2,1,0:T(8,128)(2,1)S(1)} %copy-done.9), kind=kOutput, calls=%fused_computation.26 | convolution fusion | flops 1207959552 | bytes 5898240 | tf_op jit(solution)/shard_map/fd,sf->ds/dot_general | solution.py:76
  154.2 7.8 %eq.58 = pred[512,2,2048]{2,1,0:T(4,128)(4,1)} reshape(pred[1024,2048]{1,0:T(8,128)(4,1)S(1)} %iota_compare_fusion.1) | data formatting | bytes 4194304 | tf_op jit(solution)/shard_map/eq | solution.py:33
  162.1 11.0 %reduce-scatter.9.cloned.1.call-done = f32[192,1024]{1,0:T(8,128)} async-done(((f32[768,1024]{1,0:T(8,128)}), f32[192,1024]{1,0:T(8,128)}) %reduce-scatter.9.cloned.1.call-update) | async-done | bytes 786448 | tf_op jit(solution)/shard_map/reduce_scatter | solution.py:58
  174.5 39.0 %reduce-scatter.11.cloned.1.call-done = f32[192,1024]{1,0:T(8,128)} async-done(((f32[768,1024]{1,0:T(8,128)}), f32[192,1024]{1,0:T(8,128)}) %reduce-scatter.11.cloned.1.call-update) | async-done | bytes 786448 | tf_op jit(solution)/shard_map/reduce_scatter | solution.py:58
  216.2 7.8 %all-to-all-start.3 = ((bf16[192,2,32,32]{0,3,1,2:T(8,128)(2,1)}), bf16[192,2,32,32]{0,3,1,2:T(8,128)(2,1)S(1)}, u32[]{:S(2)}, u32[]{:S(2)}) async-start(bf16[192,2,32,32]{0,3,1,2:T(8,128)(2,1)} %copy.77), calls=%async_computation.7 | async-start | bytes 2097152 | tf_op jit(solution)/shard_map/all_to_all | solution.py:69
  224.0 7.5 %convolution_convert_fusion.1 = bf16[2,768,768]{2,1,0:T(8,128)(2,1)} fusion(bf16[2,1024,768]{2,1,0:T(8,128)(2,1)} %bitcast.60, bf16[2,1024,768]{2,1,0:T(8,128)(2,1)} %copy-done.10), kind=kOutput, calls=%fused_computation.23 | convolution fusion | flops 2417098752 | bytes 8650752 | tf_op jit(solution)/shard_map/xsd,xsf->xdf/dot_general | solution.py:87
  231.4 22.5 %reduce-scatter.5.cloned.1.call-done = f32[192,1024]{1,0:T(8,128)} async-done(((f32[768,1024]{1,0:T(8,128)}), f32[192,1024]{1,0:T(8,128)}) %reduce-scatter.5.cloned.1.call-update) | async-done | bytes 786448 | tf_op jit(solution)/shard_map/reduce_scatter | solution.py:58
  255.3 38.9 %reduce-scatter.7.cloned.1.call-done = f32[192,1024]{1,0:T(8,128)} async-done(((f32[768,1024]{1,0:T(8,128)}), f32[192,1024]{1,0:T(8,128)}) %reduce-scatter.7.cloned.1.call-update) | async-done | bytes 786448 | tf_op jit(solution)/shard_map/reduce_scatter | solution.py:58
  297.0 7.8 %all-to-all-start.1 = ((bf16[192,2,32,32]{0,3,1,2:T(8,128)(2,1)}), bf16[192,2,32,32]{0,3,1,2:T(8,128)(2,1)S(1)}, u32[]{:S(2)}, u32[]{:S(2)}) async-start(bf16[192,2,32,32]{0,3,1,2:T(8,128)(2,1)} %copy.67), calls=%async_computation.3 | async-start | bytes 2097152 | tf_op jit(solution)/shard_map/all_to_all | solution.py:69
  304.7 7.1 %convolution_convert_fusion = bf16[2,768,768]{2,1,0:T(8,128)(2,1)} fusion(bf16[2,1024,768]{2,1,0:T(8,128)(2,1)} %get-tuple-element.6, bf16[2,1024,768]{2,1,0:T(8,128)(2,1)} %bitcast.58), kind=kOutput, calls=%fused_computation.22 | convolution fusion | flops 2417098752 | bytes 8650752 | tf_op jit(solution)/shard_map/xsf,xsd->xfd/dot_general | solution.py:84
  316.2 5.4 %all-to-all-done.1 = bf16[192,2,32,32]{0,3,1,2:T(8,128)(2,1)S(1)} async-done(((bf16[192,2,32,32]{0,3,1,2:T(8,128)(2,1)}), bf16[192,2,32,32]{0,3,1,2:T(8,128)(2,1)S(1)}, u32[]{:S(2)}, u32[]{:S(2)}) %all-to-all-start.1) | async-done | bytes 786464 | tf_op jit(solution)/shard_map/all_to_all | solution.py:69
  321.7 6.4 %fusion.20 = bf16[512,192]{0,1:T(8,128)(2,1)} fusion(bf16[192,2048,1]{0,1,2:T(8,128)(2,1)S(1)} %bitcast.67, pred[512,2,2048]{2,1,0:T(4,128)(4,1)} %eq.58, f32[512,2]{0,1:T(2,128)S(1)} %copy-done.5), kind=kOutput, calls=%fused_computation.34 | convolution fusion | flops 805601280 | bytes 3084288 | tf_op jit(solution)/shard_map/dot_general | solution.py:97
  (67 shorter events, 42.7 us)
Async XLA Ops:
  7.2 3.4 %copy-start.3 = (bf16[512,192]{0,1:T(8,128)(2,1)S(1)}, bf16[512,192]{0,1:T(8,128)(2,1)}, u32[]{:S(2)}) copy-start(bf16[512,192]{0,1:T(8,128)(2,1)} %param.6) | copy-start | bytes 589828
  27.4 10.5 %copy-start.4 = (bf16[512,192]{0,1:T(8,128)(2,1)S(1)}, bf16[512,192]{0,1:T(8,128)(2,1)}, u32[]{:S(2)}) copy-start(bf16[512,192]{0,1:T(8,128)(2,1)} %param.7) | copy-start | bytes 589828
  27.4 50.2 %all-to-all-start = ((bf16[2,32,32,768]{3,2,0,1:T(8,128)(2,1)}), bf16[2,32,32,768]{3,2,0,1:T(8,128)(2,1)S(1)}, u32[]{:S(2)}, u32[]{:S(2)}) async-start(bf16[2,32,32,768]{3,2,0,1:T(8,128)(2,1)} %copy.63), calls=%async_computation | async-start | bytes 6291456 | tf_op jit(solution)/shard_map/all_to_all | solution.py:46
  57.6 5.4 %copy-start.5 = (f32[512,2]{0,1:T(2,128)S(1)}, f32[512,2]{0,1:T(2,128)}, u32[]{:S(2)}) copy-start(f32[512,2]{0,1:T(2,128)} %param.8) | copy-start | bytes 12292
  77.7 45.0 %all-to-all-start.2 = ((bf16[2,32,32,768]{3,2,0,1:T(8,128)(2,1)}), bf16[2,32,32,768]{3,2,0,1:T(8,128)(2,1)}, u32[]{:S(2)}, u32[]{:S(2)}) async-start(bf16[2,32,32,768]{3,2,0,1:T(8,128)(2,1)} %copy.73), calls=%async_computation.4 | async-start | bytes 6291456 | tf_op jit(solution)/shard_map/all_to_all | solution.py:46
  82.7 90.3 %reduce-scatter.9.cloned.1.call-start = ((), (), s32[]{:S(2)}) async-start(), calls=%async_computation.10 | async-start | bytes 3932160 | tf_op jit(solution)/shard_map/reduce_scatter | solution.py:58
  83.0 2.8 copy-start.6
  83.2 1.7 copy-start.2
  122.6 2.6 copy-start.8
  124.9 6.9 %copy-start.1 = (bf16[2,32,32,768]{3,2,1,0:T(8,128)(2,1)}, bf16[2,32,32,768]{3,2,1,0:T(8,128)(2,1)S(1)}, u32[]{:S(2)}) copy-start(bf16[2,32,32,768]{3,2,1,0:T(8,128)(2,1)S(1)} %copy.74) | copy-start | bytes 9437188
  125.3 8.2 %copy-start.7 = (bf16[2,768,768]{2,1,0:T(8,128)(2,1)S(1)}, bf16[2,768,768]{2,1,0:T(8,128)(2,1)}, u32[]{:S(2)}) copy-start(bf16[2,768,768]{2,1,0:T(8,128)(2,1)} %param.10) | copy-start | bytes 7077892
  131.8 1.6 copy-start.10
  136.7 76.8 %reduce-scatter.11.cloned.1.call-start = ((), (), s32[]{:S(2)}) async-start(), calls=%async_computation.11 | async-start | bytes 3932160 | tf_op jit(solution)/shard_map/reduce_scatter | solution.py:58
  141.3 1.7 copy-start.9
  141.3 112.6 %reduce-scatter.5.cloned.1.call-start = ((), (), s32[]{:S(2)}) async-start(), calls=%async_computation.8 | async-start | bytes 3932160 | tf_op jit(solution)/shard_map/reduce_scatter | solution.py:58
  147.9 146.3 %reduce-scatter.7.cloned.1.call-start = ((), (), s32[]{:S(2)}) async-start(), calls=%async_computation.9 | async-start | bytes 3932160 | tf_op jit(solution)/shard_map/reduce_scatter | solution.py:58
  216.2 80.8 %all-to-all-start.3 = ((bf16[192,2,32,32]{0,3,1,2:T(8,128)(2,1)}), bf16[192,2,32,32]{0,3,1,2:T(8,128)(2,1)S(1)}, u32[]{:S(2)}, u32[]{:S(2)}) async-start(bf16[192,2,32,32]{0,3,1,2:T(8,128)(2,1)} %copy.77), calls=%async_computation.7 | async-start | bytes 2097152 | tf_op jit(solution)/shard_map/all_to_all | solution.py:69
  297.0 24.7 %all-to-all-start.1 = ((bf16[192,2,32,32]{0,3,1,2:T(8,128)(2,1)}), bf16[192,2,32,32]{0,3,1,2:T(8,128)(2,1)S(1)}, u32[]{:S(2)}, u32[]{:S(2)}) async-start(bf16[192,2,32,32]{0,3,1,2:T(8,128)(2,1)} %copy.67), calls=%async_computation.3 | async-start | bytes 2097152 | tf_op jit(solution)/shard_map/all_to_all | solution.py:69
  304.7 7.2 %copy-start = (pred[512,2,2048]{2,1,0:T(4,128)(4,1)S(1)}, pred[512,2,2048]{2,1,0:T(4,128)(4,1)}, u32[]{:S(2)}) copy-start(pred[512,2,2048]{2,1,0:T(4,128)(4,1)} %eq.58) | copy-start | bytes 6291460
Sparse Core Ops, SparseCore 0:
  136.8 36.2 reduce-scatter.8
  175.5 37.9 reduce-scatter.10
  215.9 37.9 reduce-scatter.4
  256.2 37.9 reduce-scatter.6
where the time goes:
time: 336 us; the launch traced here: 335 us
  waiting for transfers between devices  155 us (46%)
  matrix products  63.1 us (19%)
  local copies, waits for them, and re-layouts  37.5 us (11%)
  starting transfers between devices  31.5 us (9%)
  blocking collectives  25.9 us (8%)
  between operations  14.1 us (4%)
  other arithmetic  7.85 us (2%)
    reduce_scatter x4, waiting for transfers between devices, send_home(): lax.psum_scatter(with_layout_constraint(part, Layout((0, 1))), 'ffn', sca...  111 us
    all_to_all x2, waiting for transfers between devices, dispatch(): lax.all_to_all(send, 'expert', split_axis=1, concat_axis=1, tiled=True)  37.8 us
    all_to_all x2, starting transfers between devices, dispatch(): lax.all_to_all(send, 'expert', split_axis=1, concat_axis=1, tiled=True)  15.6 us
    all_to_all x2, starting transfers between devices, send_home(): lax.all_to_all(cols, 'expert', split_axis=2, concat_axis=2, tiled=True)  15.6 us
    all_gather x1, blocking collectives, shards(): whole_cot = lax.all_gather(cotangent, 'ffn', axis=1, tiled=True)  13 us
    all_gather x1, blocking collectives, shards(): whole_tokens = lax.all_gather(tokens, 'ffn', axis=1, tiled=True)  12.9 us
    dot_general x2, matrix products, gather_back(): lax.dot_general(placer, returned, (((0,), (1,)), ((), ())), preferred_ele...  10.7 us
    dot_general x2, matrix products, shards(): jnp.einsum('fd,sf->ds', down_weight[x], activated[x], preferred_element_t...  9.43 us
  transfers between devices with their start and end apart: 8, of which 7 were waited for; matrix products, arithmetic and copies ran while one was open for 23% of the time, Pallas kernels for 0%

commit v1 on v0

--- a/solution.py
+++ b/solution.py
@@ -56,7 +56,7 @@
         cols = jnp.stack(
             [
                 lax.psum_scatter(
-                    with_layout_constraint(part, Layout((0, 1))),
+                    with_layout_constraint(part, Layout((0, 1))).astype(jnp.bfloat16),
                     "ffn",
                     scatter_dimension=0,
                     tiled=True,

time: 336 us -> 286 us (0.85)
  waiting for transfers between devices: 155 us -> 108 us
  other arithmetic: 7.85 us -> 3.13 us
    reduce_scatter x4, waiting for transfers between devices: 111 us -> 64.6 us  [send_home(): lax.psum_scatter(with_layout_constraint(part, Layout((0, 1))).astype(jnp....]
    reduce_scatter x0 -> x4, local copies, waits for them, and re-layouts: none -> 4.79 us  [send_home(): lax.psum_scatter(with_layout_constraint(part, Layout((0, 1))).astype(jnp....]
    another operation x6 -> x2, other arithmetic: 5.13 us -> 0.41 us  [send_home(): jnp.stack([lax.psum_scatter(with_layout_constraint(part, Layout((0, 1)))....]
  transfers between devices with their start and end apart: 8 -> 8, of which waited for: 7 -> 7; matrix products, arithmetic and copies ran while one was open for 23% -> 26% of each run, Pallas kernels for 0% -> 0%
where the time goes in v1:
time: 286 us; the launch traced here: 285 us
  waiting for transfers between devices  108 us (38%)
  matrix products  60.8 us (21%)
  local copies, waits for them, and re-layouts  39.9 us (14%)
  starting transfers between devices  33.1 us (12%)
  blocking collectives  25.9 us (9%)
  between operations  14.1 us (5%)
  other arithmetic  3.13 us (1%)
    reduce_scatter x4, waiting for transfers between devices, send_home(): lax.psum_scatter(with_layout_constraint(part, Layout((0, 1))).astype(jnp....  64.6 us
    all_to_all x2, waiting for transfers between devices, dispatch(): lax.all_to_all(send, 'expert', split_axis=1, concat_axis=1, tiled=True)  37.8 us
    all_to_all x2, starting transfers between devices, send_home(): lax.all_to_all(cols, 'expert', split_axis=2, concat_axis=2, tiled=True)  17.2 us
    all_to_all x2, starting transfers between devices, dispatch(): lax.all_to_all(send, 'expert', split_axis=1, concat_axis=1, tiled=True)  15.6 us
    all_gather x1, blocking collectives, shards(): whole_cot = lax.all_gather(cotangent, 'ffn', axis=1, tiled=True)  13 us
    all_gather x1, blocking collectives, shards(): whole_tokens = lax.all_gather(tokens, 'ffn', axis=1, tiled=True)  12.9 us
    dot_general x2, matrix products, gather_back(): lax.dot_general(placer, returned, (((0,), (1,)), ((), ())), preferred_ele...  10.7 us
    dot_general x2, matrix products, shards(): jnp.einsum('fd,sf->ds', down_weight[x], activated[x], preferred_element_t...  8.48 us
  transfers between devices with their start and end apart: 8, of which 7 were waited for; matrix products, arithmetic and copies ran while one was open for 26% of the time, Pallas kernels for 0%

profile of v1, /device:TPU:1, one launch (start us, length us, event | category | flops | bytes accessed | tf_op | source)
XLA Modules:
  0.0 284.7 jit_solution(7166120425335047132)
XLA Ops:
  10.5 12.9 %all_gather.6 = bf16[512,768]{0,1:T(8,128)(2,1)S(1)} all-gather(bf16[512,192]{0,1:T(8,128)(2,1)S(1)} %copy-done.3), channel_id=1, replica_groups=mesh['expert'=32,'ffn'=4] {'ffn'}, dimensions={1}, use_global_device_ids=true | all-gather | bytes 983040 | tf_op jit(solution)/shard_map/all_gather | solution.py:41
  27.4 10.5 %all-to-all-start = ((bf16[2,32,32,768]{3,2,0,1:T(8,128)(2,1)}), bf16[2,32,32,768]{3,2,0,1:T(8,128)(2,1)S(1)}, u32[]{:S(2)}, u32[]{:S(2)}) async-start(bf16[2,32,32,768]{3,2,0,1:T(8,128)(2,1)} %copy.63), calls=%async_computation | async-start | bytes 6291456 | tf_op jit(solution)/shard_map/all_to_all | solution.py:46
  37.9 13.0 %all_gather.7 = bf16[512,768]{0,1:T(8,128)(2,1)} all-gather(bf16[512,192]{0,1:T(8,128)(2,1)S(1)} %copy-done.4), channel_id=1, replica_groups=mesh['expert'=32,'ffn'=4] {'ffn'}, dimensions={1}, use_global_device_ids=true | all-gather | bytes 983040 | tf_op jit(solution)/shard_map/all_gather | solution.py:42
  53.5 4.2 %broadcast_in_dim.2 = f32[512,2,768]{2,1,0:T(2,128)} broadcast(f32[512,768]{1,0:T(8,128)} %copy.72), dimensions={0,2} | broadcast | bytes 4718592 | tf_op jit(solution)/shard_map/broadcast_in_dim | solution.py:50
  57.6 5.4 %convert_element_type.76 = f32[1024,768]{1,0:T(8,128)} reshape(f32[512,2,768]{2,1,0:T(2,128)} %broadcast_in_dim.2) | data formatting | bytes 6291456 | tf_op jit(solution)/shard_map/convert_element_type | solution.py:50
  63.3 6.0 %fusion.9 = bf16[2048,768]{1,0:T(8,128)(2,1)S(1)} fusion(s32[1024]{0:T(1024)S(1)} %fusion.48, f32[1024,768]{1,0:T(8,128)} %convert_element_type.76, f32[1024]{0:T(1024)S(1)} %mul.75), kind=kOutput, calls=%fused_computation.14 | convolution fusion | flops 3226468352 | bytes 6299648 | tf_op jit(solution)/shard_map/dot_general | solution.py:53
  71.4 6.3 %all-to-all-done = bf16[2,32,32,768]{3,2,0,1:T(8,128)(2,1)S(1)} async-done(((bf16[2,32,32,768]{3,2,0,1:T(8,128)(2,1)}), bf16[2,32,32,768]{3,2,0,1:T(8,128)(2,1)S(1)}, u32[]{:S(2)}, u32[]{:S(2)}) %all-to-all-start) | async-done | bytes 3145760 | tf_op jit(solution)/shard_map/all_to_all | solution.py:46
  77.7 5.1 %all-to-all-start.2 = ((bf16[2,32,32,768]{3,2,0,1:T(8,128)(2,1)}), bf16[2,32,32,768]{3,2,0,1:T(8,128)(2,1)}, u32[]{:S(2)}, u32[]{:S(2)}) async-start(bf16[2,32,32,768]{3,2,0,1:T(8,128)(2,1)} %copy.73), calls=%async_computation.4 | async-start | bytes 6291456 | tf_op jit(solution)/shard_map/all_to_all | solution.py:46
  85.7 5.4 %multiply_convert_fusion.1 = (bf16[2,1024,768]{2,1,0:T(8,128)(2,1)}, f32[2,1024,768]{2,1,0:T(8,128)}) fusion(bf16[2,1024,768]{2,1,0:T(8,128)(2,1)S(1)} %bitcast.59, bf16[2,768,768]{2,1,0:T(8,128)(2,1)S(1)} %copy-done.6), kind=kOutput, calls=%fused_computation.4 | convolution fusion | flops 2423783424 | bytes 14942208 | tf_op jit(solution)/shard_map/xsd,xdf->xsf/dot_general | solution.py:72
  91.1 31.5 %all-to-all-done.2 = bf16[2,32,32,768]{3,2,0,1:T(8,128)(2,1)} async-done(((bf16[2,32,32,768]{3,2,0,1:T(8,128)(2,1)}), bf16[2,32,32,768]{3,2,0,1:T(8,128)(2,1)}, u32[]{:S(2)}, u32[]{:S(2)}) %all-to-all-start.2) | async-done | bytes 3145760 | tf_op jit(solution)/shard_map/all_to_all | solution.py:46
  125.3 6.6 %multiply_convert_fusion = bf16[2,1024,768]{2,1,0:T(8,128)(2,1)S(1)} fusion(f32[2,1024,768]{2,1,0:T(8,128)} %get-tuple-element.7, bf16[2,1024,768]{2,1,0:T(8,128)(2,1)S(1)} %bitcast.57, bf16[2,768,768]{2,1,0:T(8,128)(2,1)S(1)} %copy-done.8), kind=kOutput, calls=%fused_computation.3 | convolution fusion | flops 2430074880 | bytes 14942208 | tf_op jit(solution)/shard_map/xsd,xfd->xsf/dot_general | solution.py:80
  140.2 4.5 %bitcast_convert_fusion.3 = bf16[768,1024]{1,0:T(8,128)(2,1)} fusion(bf16[2,1024,768]{2,1,0:T(8,128)(2,1)} %get-tuple-element.6, bf16[2,768,768]{2,1,0:T(8,128)(2,1)} %param.11), kind=kOutput, calls=%fused_computation.18 | convolution fusion | flops 1208745984 | bytes 4325376 | tf_op jit(solution)/shard_map/fd,sf->ds/dot_general | solution.py:76
  144.8 4.0 %bitcast_convert_fusion.2 = bf16[768,1024]{1,0:T(8,128)(2,1)} fusion(bf16[2,1024,768]{2,1,0:T(8,128)(2,1)} %get-tuple-element.6, bf16[2,768,768]{2,1,0:T(8,128)(2,1)S(1)} %copy-done.9), kind=kOutput, calls=%fused_computation.17 | convolution fusion | flops 1208745984 | bytes 4325376 | tf_op jit(solution)/shard_map/fd,sf->ds/dot_general | solution.py:76
  150.5 7.8 %eq.58 = pred[512,2,2048]{2,1,0:T(4,128)(4,1)} reshape(pred[1024,2048]{1,0:T(8,128)(4,1)S(1)} %iota_compare_fusion.1) | data formatting | bytes 4194304 | tf_op jit(solution)/shard_map/eq | solution.py:33
  160.3 27.2 %reduce-scatter.11.cloned.1.call-done = bf16[192,1024]{1,0:T(8,128)(2,1)} async-done(((bf16[768,1024]{1,0:T(8,128)(2,1)}), bf16[192,1024]{1,0:T(8,128)(2,1)}) %reduce-scatter.11.cloned.1.call-update) | async-done | bytes 393232 | tf_op jit(solution)/shard_map/reduce_scatter | solution.py:58
  190.0 8.6 %all-to-all-start.3 = ((bf16[192,2,32,32]{0,3,1,2:T(8,128)(2,1)}), bf16[192,2,32,32]{0,3,1,2:T(8,128)(2,1)S(1)}, u32[]{:S(2)}, u32[]{:S(2)}) async-start(bf16[192,2,32,32]{0,3,1,2:T(8,128)(2,1)} %copy.77), calls=%async_computation.7 | async-start | bytes 2097152 | tf_op jit(solution)/shard_map/all_to_all | solution.py:69
  198.6 7.2 %convolution_convert_fusion.1 = bf16[2,768,768]{2,1,0:T(8,128)(2,1)} fusion(bf16[2,1024,768]{2,1,0:T(8,128)(2,1)} %bitcast.60, bf16[2,1024,768]{2,1,0:T(8,128)(2,1)} %copy-done.10), kind=kOutput, calls=%fused_computation.27 | convolution fusion | flops 2417098752 | bytes 8650752 | tf_op jit(solution)/shard_map/xsd,xsf->xdf/dot_general | solution.py:87
  205.8 9.5 %reduce-scatter.5.cloned.1.call-done = bf16[192,1024]{1,0:T(8,128)(2,1)} async-done(((bf16[768,1024]{1,0:T(8,128)(2,1)}), bf16[192,1024]{1,0:T(8,128)(2,1)}) %reduce-scatter.5.cloned.1.call-update) | async-done | bytes 393232 | tf_op jit(solution)/shard_map/reduce_scatter | solution.py:58
  216.6 27.1 %reduce-scatter.7.cloned.1.call-done = bf16[192,1024]{1,0:T(8,128)(2,1)} async-done(((bf16[768,1024]{1,0:T(8,128)(2,1)}), bf16[192,1024]{1,0:T(8,128)(2,1)}) %reduce-scatter.7.cloned.1.call-update) | async-done | bytes 393232 | tf_op jit(solution)/shard_map/reduce_scatter | solution.py:58
  246.1 8.6 %all-to-all-start.1 = ((bf16[192,2,32,32]{0,3,1,2:T(8,128)(2,1)}), bf16[192,2,32,32]{0,3,1,2:T(8,128)(2,1)S(1)}, u32[]{:S(2)}, u32[]{:S(2)}) async-start(bf16[192,2,32,32]{0,3,1,2:T(8,128)(2,1)} %copy.67), calls=%async_computation.3 | async-start | bytes 2097152 | tf_op jit(solution)/shard_map/all_to_all | solution.py:69
  254.7 7.1 %convolution_convert_fusion = bf16[2,768,768]{2,1,0:T(8,128)(2,1)} fusion(bf16[2,1024,768]{2,1,0:T(8,128)(2,1)} %get-tuple-element.6, bf16[2,1024,768]{2,1,0:T(8,128)(2,1)} %bitcast.58), kind=kOutput, calls=%fused_computation.26 | convolution fusion | flops 2417098752 | bytes 8650752 | tf_op jit(solution)/shard_map/xsf,xsd->xfd/dot_general | solution.py:84
  261.9 4.3 %fusion.23 = bf16[512,192]{0,1:T(8,128)(2,1)} fusion(bf16[192,2048,1]{0,1,2:T(8,128)(2,1)S(1)} %bitcast.68, pred[512,2,2048]{2,1,0:T(4,128)(4,1)S(1)} %copy-done), kind=kOutput, calls=%fused_computation.35 | convolution fusion | flops 805404672 | bytes 3080192 | tf_op jit(solution)/shard_map/dot_general | solution.py:97
  266.2 5.4 %all-to-all-done.1 = bf16[192,2,32,32]{0,3,1,2:T(8,128)(2,1)S(1)} async-done(((bf16[192,2,32,32]{0,3,1,2:T(8,128)(2,1)}), bf16[192,2,32,32]{0,3,1,2:T(8,128)(2,1)S(1)}, u32[]{:S(2)}, u32[]{:S(2)}) %all-to-all-start.1) | async-done | bytes 786464 | tf_op jit(solution)/shard_map/all_to_all | solution.py:69
  271.7 6.4 %fusion.20 = bf16[512,192]{0,1:T(8,128)(2,1)} fusion(bf16[192,2048,1]{0,1,2:T(8,128)(2,1)S(1)} %bitcast.67, pred[512,2,2048]{2,1,0:T(4,128)(4,1)} %eq.58, f32[512,2]{0,1:T(2,128)S(1)} %copy-done.5), kind=kOutput, calls=%fused_computation.34 | convolution fusion | flops 805601280 | bytes 3084288 | tf_op jit(solution)/shard_map/dot_general | solution.py:97
  (63 shorter events, 36.1 us)
Async XLA Ops:
  7.2 3.4 %copy-start.3 = (bf16[512,192]{0,1:T(8,128)(2,1)S(1)}, bf16[512,192]{0,1:T(8,128)(2,1)}, u32[]{:S(2)}) copy-start(bf16[512,192]{0,1:T(8,128)(2,1)} %param.6) | copy-start | bytes 589828
  27.4 10.5 %copy-start.4 = (bf16[512,192]{0,1:T(8,128)(2,1)S(1)}, bf16[512,192]{0,1:T(8,128)(2,1)}, u32[]{:S(2)}) copy-start(bf16[512,192]{0,1:T(8,128)(2,1)} %param.7) | copy-start | bytes 589828
  27.4 50.2 %all-to-all-start = ((bf16[2,32,32,768]{3,2,0,1:T(8,128)(2,1)}), bf16[2,32,32,768]{3,2,0,1:T(8,128)(2,1)S(1)}, u32[]{:S(2)}, u32[]{:S(2)}) async-start(bf16[2,32,32,768]{3,2,0,1:T(8,128)(2,1)} %copy.63), calls=%async_computation | async-start | bytes 6291456 | tf_op jit(solution)/shard_map/all_to_all | solution.py:46
  57.6 5.4 %copy-start.5 = (f32[512,2]{0,1:T(2,128)S(1)}, f32[512,2]{0,1:T(2,128)}, u32[]{:S(2)}) copy-start(f32[512,2]{0,1:T(2,128)} %param.8) | copy-start | bytes 12292
  77.7 45.0 %all-to-all-start.2 = ((bf16[2,32,32,768]{3,2,0,1:T(8,128)(2,1)}), bf16[2,32,32,768]{3,2,0,1:T(8,128)(2,1)}, u32[]{:S(2)}, u32[]{:S(2)}) async-start(bf16[2,32,32,768]{3,2,0,1:T(8,128)(2,1)} %copy.73), calls=%async_computation.4 | async-start | bytes 6291456 | tf_op jit(solution)/shard_map/all_to_all | solution.py:46
  82.7 76.3 %reduce-scatter.9.cloned.1.call-start = ((), (), s32[]{:S(2)}) async-start(), calls=%async_computation.10 | async-start | bytes 1966080 | tf_op jit(solution)/shard_map/reduce_scatter | solution.py:58
  83.0 2.8 copy-start.6
  83.2 1.7 copy-start.2
  122.6 2.6 copy-start.8
  124.9 6.9 %copy-start.1 = (bf16[2,32,32,768]{3,2,1,0:T(8,128)(2,1)}, bf16[2,32,32,768]{3,2,1,0:T(8,128)(2,1)S(1)}, u32[]{:S(2)}) copy-start(bf16[2,32,32,768]{3,2,1,0:T(8,128)(2,1)S(1)} %copy.74) | copy-start | bytes 9437188
  125.3 8.2 %copy-start.7 = (bf16[2,768,768]{2,1,0:T(8,128)(2,1)S(1)}, bf16[2,768,768]{2,1,0:T(8,128)(2,1)}, u32[]{:S(2)}) copy-start(bf16[2,768,768]{2,1,0:T(8,128)(2,1)} %param.10) | copy-start | bytes 7077892
  131.8 1.6 copy-start.10
  136.1 51.4 %reduce-scatter.11.cloned.1.call-start = ((), (), s32[]{:S(2)}) async-start(), calls=%async_computation.11 | async-start | bytes 1966080 | tf_op jit(solution)/shard_map/reduce_scatter | solution.py:58
  140.1 75.2 %reduce-scatter.5.cloned.1.call-start = ((), (), s32[]{:S(2)}) async-start(), calls=%async_computation.8 | async-start | bytes 1966080 | tf_op jit(solution)/shard_map/reduce_scatter | solution.py:58
  140.2 4.6 %copy-start.9 = (bf16[2,768,768]{2,1,0:T(8,128)(2,1)S(1)}, bf16[2,768,768]{2,1,0:T(8,128)(2,1)}, u32[]{:S(2)}) copy-start(bf16[2,768,768]{2,1,0:T(8,128)(2,1)} %param.11) | copy-start | bytes 7077892
  144.7 98.9 %reduce-scatter.7.cloned.1.call-start = ((), (), s32[]{:S(2)}) async-start(), calls=%async_computation.9 | async-start | bytes 1966080 | tf_op jit(solution)/shard_map/reduce_scatter | solution.py:58
  190.0 56.2 %all-to-all-start.3 = ((bf16[192,2,32,32]{0,3,1,2:T(8,128)(2,1)}), bf16[192,2,32,32]{0,3,1,2:T(8,128)(2,1)S(1)}, u32[]{:S(2)}, u32[]{:S(2)}) async-start(bf16[192,2,32,32]{0,3,1,2:T(8,128)(2,1)} %copy.77), calls=%async_computation.7 | async-start | bytes 2097152 | tf_op jit(solution)/shard_map/all_to_all | solution.py:69
  246.1 25.5 %all-to-all-start.1 = ((bf16[192,2,32,32]{0,3,1,2:T(8,128)(2,1)}), bf16[192,2,32,32]{0,3,1,2:T(8,128)(2,1)S(1)}, u32[]{:S(2)}, u32[]{:S(2)}) async-start(bf16[192,2,32,32]{0,3,1,2:T(8,128)(2,1)} %copy.67), calls=%async_computation.3 | async-start | bytes 2097152 | tf_op jit(solution)/shard_map/all_to_all | solution.py:69
  254.7 7.2 %copy-start = (pred[512,2,2048]{2,1,0:T(4,128)(4,1)S(1)}, pred[512,2,2048]{2,1,0:T(4,128)(4,1)}, u32[]{:S(2)}) copy-start(pred[512,2,2048]{2,1,0:T(4,128)(4,1)} %eq.58) | copy-start | bytes 6291460
Sparse Core Ops, SparseCore 0:
  136.2 22.8 reduce-scatter.8
  162.0 25.3 reduce-scatter.10
  189.9 25.3 reduce-scatter.4
  218.2 25.3 reduce-scatter.6

commit v2 on v1

--- a/solution.py
+++ b/solution.py
@@ -38,8 +38,10 @@
     )
     weights = gates.reshape(-1)
 
-    whole_tokens = lax.all_gather(tokens, "ffn", axis=1, tiled=True)
-    whole_cot = lax.all_gather(cotangent, "ffn", axis=1, tiled=True)
+    width = tokens.shape[1]
+    both = lax.all_gather(jnp.concatenate([tokens, cotangent], axis=1), "ffn", axis=1)
+    whole_tokens = both[:, :, :width].reshape(tok_rows, -1)
+    whole_cot = both[:, :, width:].reshape(tok_rows, -1)
 
     def dispatch(send):
         send = send.astype(jnp.bfloat16).reshape(local_experts, owners, capacity, send.shape[1])
@@ -47,24 +49,19 @@
         return got.reshape(local_experts, slots, got.shape[3])
 
     rows_in = dispatch(jnp.dot(token_placer, whole_tokens, preferred_element_type=jnp.float32))
-    assigned = (weights[:, None] * jnp.repeat(whole_cot, 2, axis=0).astype(jnp.float32)).astype(
-        jnp.bfloat16
-    )
+    assigned = (gates[:, :, None] * whole_cot[:, None, :].astype(jnp.float32)).astype(jnp.bfloat16)
+    assigned = assigned.reshape(2 * tok_rows, whole_cot.shape[1])
     grads_in = dispatch(jnp.dot(placer, assigned, preferred_element_type=jnp.float32))
 
     def send_home(parts):
-        cols = jnp.stack(
-            [
-                lax.psum_scatter(
-                    with_layout_constraint(part, Layout((0, 1))).astype(jnp.bfloat16),
-                    "ffn",
-                    scatter_dimension=0,
-                    tiled=True,
-                )
-                for part in parts
-            ],
+        ffn = lax.axis_size("ffn")
+        stacked = jnp.stack(
+            [with_layout_constraint(part, Layout((0, 1))).astype(jnp.bfloat16) for part in parts],
             axis=1,
-        ).astype(jnp.bfloat16)
+        )
+        stacked = stacked.reshape(ffn, stacked.shape[0] // ffn, local_experts, slots)
+        pieces = lax.all_to_all(stacked, "ffn", split_axis=0, concat_axis=0, tiled=True)
+        cols = jnp.sum(pieces.astype(jnp.float32), axis=0).astype(jnp.bfloat16)
         cols = cols.reshape(cols.shape[0], local_experts, owners, capacity)
         back = lax.all_to_all(cols, "expert", split_axis=2, concat_axis=2, tiled=True)
         return back.reshape(back.shape[0], rows)

time: 286 us -> 322 us (1.13)
  waiting for transfers between devices: 108 us -> 137 us
  blocking collectives: 25.9 us -> 0 us
  other arithmetic: 3.13 us -> 17.2 us
  starting transfers between devices: 33.1 us -> 46 us
  local copies, waits for them, and re-layouts: 39.9 us -> 49.5 us
  matrix products: 60.8 us -> 53.4 us
    reduce_scatter x4 -> x0, waiting for transfers between devices: 64.6 us -> none  [send_home(): lax.psum_scatter(with_layout_constraint(part, Layout((0, 1))).astype(jnp....]
    all_to_all x0 -> x2, waiting for transfers between devices: none -> 57.9 us  [send_home(): lax.all_to_all(stacked, 'ffn', split_axis=0, concat_axis=0, tiled=True)]
    all_gather x0 -> x1, waiting for transfers between devices: none -> 27.4 us  [shards(): lax.all_gather(jnp.concatenate([tokens, cotangent], axis=1), 'ffn', axis=1)]
    all_gather x2 -> x0, blocking collectives: 25.9 us -> none  [the longest x1 13 us: shards(): whole_cot = lax.all_gather(cotangent, 'ffn', axis=1, tiled=True)]
    all_to_all x2, waiting for transfers between devices: 37.8 us -> 47.8 us  [dispatch(): lax.all_to_all(send, 'expert', split_axis=1, concat_axis=1, tiled=True)]
    mul x1 -> x3, local copies, waits for them, and re-layouts: 0.17 us -> 9.7 us  [shards(): gates[:, :, None] * whole_cot[:, None, :].astype(jnp.float32)]
    all_to_all x2, starting transfers between devices: 17.2 us -> 25.1 us  [send_home(): lax.all_to_all(cols, 'expert', split_axis=2, concat_axis=2, tiled=True)]
    all_to_all x0 -> x2, starting transfers between devices: none -> 7.4 us  [send_home(): lax.all_to_all(stacked, 'ffn', split_axis=0, concat_axis=0, tiled=True)]
  transfers between devices with their start and end apart: 8 -> 7, of which waited for: 7 -> 6; matrix products, arithmetic and copies ran while one was open for 26% -> 27% of each run, Pallas kernels for 0% -> 0%
where the time goes in v2:
time: 322 us; the launch traced here: 318 us
  waiting for transfers between devices  137 us (43%)
  matrix products  53.4 us (17%)
  local copies, waits for them, and re-layouts  49.5 us (15%)
  starting transfers between devices  46 us (14%)
  other arithmetic  17.2 us (5%)
  between operations  14.5 us (5%)
    all_to_all x2, waiting for transfers between devices, send_home(): lax.all_to_all(stacked, 'ffn', split_axis=0, concat_axis=0, tiled=True)  57.9 us
    all_to_all x2, waiting for transfers between devices, dispatch(): lax.all_to_all(send, 'expert', split_axis=1, concat_axis=1, tiled=True)  47.8 us
    all_gather x1, waiting for transfers between devices, shards(): lax.all_gather(jnp.concatenate([tokens, cotangent], axis=1), 'ffn', axis=1)  27.4 us
    all_to_all x2, starting transfers between devices, send_home(): lax.all_to_all(cols, 'expert', split_axis=2, concat_axis=2, tiled=True)  25.1 us
    all_to_all x2, starting transfers between devices, dispatch(): lax.all_to_all(send, 'expert', split_axis=1, concat_axis=1, tiled=True)  13.5 us
    eq x1, local copies, waits for them, and re-layouts, shards(): placer = (row_ids == target[None, :]).astype(jnp.bfloat16)  13.4 us
    dot_general x2, matrix products, gather_back(): lax.dot_general(placer, returned, (((0,), (1,)), ((), ())), preferred_ele...  10.7 us
    mul x3, local copies, waits for them, and re-layouts, shards(): gates[:, :, None] * whole_cot[:, None, :].astype(jnp.float32)  9.7 us
  transfers between devices with their start and end apart: 7, of which 6 were waited for; matrix products, arithmetic and copies ran while one was open for 27% of the time, Pallas kernels for 0%

profile of v2, /device:TPU:1, one launch (start us, length us, event | category | flops | bytes accessed | tf_op | source)
XLA Modules:
  0.0 317.9 jit_solution(13697227018098338515)
XLA Ops:
  12.3 27.4 %all-gather.3.cloned.1.call-done = bf16[512,1536]{0,1:T(8,128)(2,1)} async-done(((bf16[512,384]{0,1:T(8,128)(2,1)}), bf16[512,1536]{0,1:T(8,128)(2,1)}) %all-gather.3.cloned.1.call-update) | async-done | bytes 1572880 | tf_op jit(solution)/shard_map/all_gather | solution.py:42
  46.1 8.0 %all-to-all-start = ((bf16[2,32,32,768]{3,2,0,1:T(8,128)(2,1)}), bf16[2,32,32,768]{3,2,0,1:T(8,128)(2,1)S(1)}, u32[]{:S(2)}, u32[]{:S(2)}) async-start(bf16[2,32,32,768]{3,2,0,1:T(8,128)(2,1)} %copy.53), calls=%async_computation | async-start | bytes 6291456 | tf_op jit(solution)/shard_map/all_to_all | solution.py:48
  60.0 4.2 %mul.85 = f32[512,2,768]{2,1,0:T(2,128)} broadcast(f32[512,768]{1,0:T(8,128)} %copy.64), dimensions={0,2} | broadcast | bytes 4718592 | tf_op jit(solution)/shard_map/mul | solution.py:52
  64.1 5.3 %mul.86 = f32[1024,768]{1,0:T(8,128)} reshape(f32[512,2,768]{2,1,0:T(2,128)} %mul.85) | data formatting | bytes 6291456 | tf_op jit(solution)/shard_map/mul | solution.py:52
  69.5 6.0 %fusion.9 = bf16[2048,768]{1,0:T(8,128)(2,1)S(1)} fusion(s32[1024]{0:T(1024)S(1)} %fusion.48, f32[1024,768]{1,0:T(8,128)} %mul.86, f32[1024]{0:T(1024)S(1)} %mul.83), kind=kOutput, calls=%fused_computation.14 | convolution fusion | flops 3226468352 | bytes 6299648 | tf_op jit(solution)/shard_map/dot_general | solution.py:54
  77.5 16.4 %all-to-all-done = bf16[2,32,32,768]{3,2,0,1:T(8,128)(2,1)S(1)} async-done(((bf16[2,32,32,768]{3,2,0,1:T(8,128)(2,1)}), bf16[2,32,32,768]{3,2,0,1:T(8,128)(2,1)S(1)}, u32[]{:S(2)}, u32[]{:S(2)}) %all-to-all-start) | async-done | bytes 3145760 | tf_op jit(solution)/shard_map/all_to_all | solution.py:48
  93.8 5.5 %all-to-all-start.3 = ((bf16[2,32,32,768]{3,2,0,1:T(8,128)(2,1)}), bf16[2,32,32,768]{3,2,0,1:T(8,128)(2,1)}, u32[]{:S(2)}, u32[]{:S(2)}) async-start(bf16[2,32,32,768]{3,2,0,1:T(8,128)(2,1)} %copy.65), calls=%async_computation.3 | async-start | bytes 6291456 | tf_op jit(solution)/shard_map/all_to_all | solution.py:48
  102.1 5.4 %multiply_convert_fusion.1 = (bf16[2,1024,768]{2,1,0:T(8,128)(2,1)}, f32[2,1024,768]{2,1,0:T(8,128)}) fusion(bf16[2,1024,768]{2,1,0:T(8,128)(2,1)S(1)} %bitcast.74, bf16[2,768,768]{2,1,0:T(8,128)(2,1)S(1)} %copy-done.5), kind=kOutput, calls=%fused_computation.4 | convolution fusion | flops 2423783424 | bytes 14942208 | tf_op jit(solution)/shard_map/xsd,xdf->xsf/dot_general | solution.py:69
  107.5 31.4 %all-to-all-done.3 = bf16[2,32,32,768]{3,2,0,1:T(8,128)(2,1)} async-done(((bf16[2,32,32,768]{3,2,0,1:T(8,128)(2,1)}), bf16[2,32,32,768]{3,2,0,1:T(8,128)(2,1)}, u32[]{:S(2)}, u32[]{:S(2)}) %all-to-all-start.3) | async-done | bytes 3145760 | tf_op jit(solution)/shard_map/all_to_all | solution.py:48
  141.2 6.9 %multiply_convert_fusion = bf16[2,1024,768]{2,1,0:T(8,128)(2,1)S(1)} fusion(f32[2,1024,768]{2,1,0:T(8,128)} %get-tuple-element.9, bf16[2,1024,768]{2,1,0:T(8,128)(2,1)S(1)} %bitcast.76, bf16[2,768,768]{2,1,0:T(8,128)(2,1)S(1)} %copy-done.7), kind=kOutput, calls=%fused_computation.3 | convolution fusion | flops 2430074880 | bytes 14942208 | tf_op jit(solution)/shard_map/xsd,xfd->xsf/dot_general | solution.py:77
  153.1 3.7 %all-to-all-start.4 = ((bf16[4,192,2,1024]{3,1,2,0:T(8,128)(2,1)}), bf16[4,192,2,1024]{3,1,2,0:T(8,128)(2,1)S(1)}, u32[]{:S(2)}, u32[]{:S(2)}) async-start(bf16[4,192,2,1024]{3,1,2,0:T(8,128)(2,1)} %pad_maximum_fusion.1), calls=%async_computation.4 | async-start | bytes 6291456 | tf_op jit(solution)/shard_map/all_to_all | solution.py:63
  156.9 3.3 %bitcast_convert_fusion.2 = bf16[768,1024]{1,0:T(8,128)(2,1)S(1)} fusion(bf16[2,1024,768]{2,1,0:T(8,128)(2,1)} %get-tuple-element.8, bf16[2,768,768]{2,1,0:T(8,128)(2,1)} %param.11), kind=kOutput, calls=%fused_computation.19 | convolution fusion | flops 1208745984 | bytes 4325376 | tf_op jit(solution)/shard_map/fd,sf->ds/dot_general | solution.py:73
  163.6 30.0 %all-to-all-done.4 = bf16[4,192,2,1024]{3,1,2,0:T(8,128)(2,1)S(1)} async-done(((bf16[4,192,2,1024]{3,1,2,0:T(8,128)(2,1)}), bf16[4,192,2,1024]{3,1,2,0:T(8,128)(2,1)S(1)}, u32[]{:S(2)}, u32[]{:S(2)}) %all-to-all-start.4) | async-done | bytes 3145760 | tf_op jit(solution)/shard_map/all_to_all | solution.py:63
  195.4 3.7 %all-to-all-start.1 = ((bf16[4,192,2,1024]{3,1,2,0:T(8,128)(2,1)}), bf16[4,192,2,1024]{3,1,2,0:T(8,128)(2,1)S(1)}, u32[]{:S(2)}, u32[]{:S(2)}) async-start(bf16[4,192,2,1024]{3,1,2,0:T(8,128)(2,1)} %pad_maximum_fusion), calls=%async_computation.1 | async-start | bytes 6291456 | tf_op jit(solution)/shard_map/all_to_all | solution.py:63
  199.1 3.6 %reduce_sum.54 = bf16[192,2,1024]{2,0,1:T(8,128)(2,1)} reduce(bf16[4,192,2,1024]{3,1,2,0:T(8,128)(2,1)} %copy-done, bf16[]{:T(256)} %constant.38.clone.1), dimensions={0}, to_apply=%region_3.4 | reduce | flops 1179648 | bytes 3932162 | tf_op jit(solution)/shard_map/reduce_sum | solution.py:64
  207.2 27.9 %all-to-all-done.1 = bf16[4,192,2,1024]{3,1,2,0:T(8,128)(2,1)S(1)} async-done(((bf16[4,192,2,1024]{3,1,2,0:T(8,128)(2,1)}), bf16[4,192,2,1024]{3,1,2,0:T(8,128)(2,1)S(1)}, u32[]{:S(2)}, u32[]{:S(2)}) %all-to-all-start.1) | async-done | bytes 3145760 | tf_op jit(solution)/shard_map/all_to_all | solution.py:63
  235.1 17.6 %all-to-all-start.5 = ((bf16[192,2,32,32]{0,3,1,2:T(8,128)(2,1)}), bf16[192,2,32,32]{0,3,1,2:T(8,128)(2,1)}, u32[]{:S(2)}, u32[]{:S(2)}) async-start(bf16[192,2,32,32]{0,3,1,2:T(8,128)(2,1)} %copy.71), calls=%async_computation.5 | async-start | bytes 2097152 | tf_op jit(solution)/shard_map/all_to_all | solution.py:66
  255.3 13.4 %eq.58 = pred[512,2,2048]{2,1,0:T(4,128)(4,1)} reshape(pred[1024,2048]{1,0:T(8,128)(4,1)} %iota_compare_fusion.1) | data formatting | bytes 4194304 | tf_op jit(solution)/shard_map/eq | solution.py:33
  268.7 7.0 %convolution_convert_fusion = bf16[2,768,768]{2,1,0:T(8,128)(2,1)} fusion(bf16[2,1024,768]{2,1,0:T(8,128)(2,1)} %get-tuple-element.8, bf16[2,1024,768]{2,1,0:T(8,128)(2,1)} %bitcast.77), kind=kOutput, calls=%fused_computation.28 | convolution fusion | flops 2417098752 | bytes 8650752 | tf_op jit(solution)/shard_map/xsf,xsd->xfd/dot_general | solution.py:81
  280.0 7.5 %all-to-all-start.2 = ((bf16[192,2,32,32]{0,3,1,2:T(8,128)(2,1)}), bf16[192,2,32,32]{0,3,1,2:T(8,128)(2,1)S(1)}, u32[]{:S(2)}, u32[]{:S(2)}) async-start(bf16[192,2,32,32]{0,3,1,2:T(8,128)(2,1)} %copy.59), calls=%async_computation.2 | async-start | bytes 2097152 | tf_op jit(solution)/shard_map/all_to_all | solution.py:66
  287.5 7.1 %convolution_convert_fusion.1 = bf16[2,768,768]{2,1,0:T(8,128)(2,1)} fusion(bf16[2,1024,768]{2,1,0:T(8,128)(2,1)} %bitcast.75, bf16[2,1024,768]{2,1,0:T(8,128)(2,1)} %copy-done.10), kind=kOutput, calls=%fused_computation.29 | convolution fusion | flops 2417098752 | bytes 8650752 | tf_op jit(solution)/shard_map/xsd,xsf->xdf/dot_general | solution.py:84
  295.9 4.3 %fusion.23 = bf16[512,192]{0,1:T(8,128)(2,1)} fusion(bf16[192,2048,1]{0,1,2:T(8,128)(2,1)S(1)} %bitcast.86, pred[512,2,2048]{2,1,0:T(4,128)(4,1)S(1)} %copy-done.1), kind=kOutput, calls=%fused_computation.37 | convolution fusion | flops 805404672 | bytes 3080192 | tf_op jit(solution)/shard_map/dot_general | solution.py:94
  300.2 4.2 %all-to-all-done.2 = bf16[192,2,32,32]{0,3,1,2:T(8,128)(2,1)S(1)} async-done(((bf16[192,2,32,32]{0,3,1,2:T(8,128)(2,1)}), bf16[192,2,32,32]{0,3,1,2:T(8,128)(2,1)S(1)}, u32[]{:S(2)}, u32[]{:S(2)}) %all-to-all-start.2) | async-done | bytes 786464 | tf_op jit(solution)/shard_map/all_to_all | solution.py:66
  304.5 6.4 %fusion.20 = bf16[512,192]{0,1:T(8,128)(2,1)} fusion(bf16[192,2048,1]{0,1,2:T(8,128)(2,1)S(1)} %bitcast.85, pred[512,2,2048]{2,1,0:T(4,128)(4,1)} %eq.58, f32[512,2]{0,1:T(2,128)S(1)} %copy-done.4), kind=kOutput, calls=%fused_computation.36 | convolution fusion | flops 805601280 | bytes 3084288 | tf_op jit(solution)/shard_map/dot_general | solution.py:94
  (59 shorter events, 47.2 us)
Async XLA Ops:
  7.2 32.5 %all-gather.3.cloned.1.call-start = ((), (), s32[]{:S(2)}) async-start(), calls=%async_computation.6 | async-start | bytes 1966080 | tf_op jit(solution)/shard_map/all_gather | solution.py:42
  46.1 8.0 %copy-start.4 = (f32[512,2]{0,1:T(2,128)S(1)}, f32[512,2]{0,1:T(2,128)}, u32[]{:S(2)}) copy-start(f32[512,2]{0,1:T(2,128)} %param.8) | copy-start | bytes 12292
  46.1 47.7 %all-to-all-start = ((bf16[2,32,32,768]{3,2,0,1:T(8,128)(2,1)}), bf16[2,32,32,768]{3,2,0,1:T(8,128)(2,1)S(1)}, u32[]{:S(2)}, u32[]{:S(2)}) async-start(bf16[2,32,32,768]{3,2,0,1:T(8,128)(2,1)} %copy.53), calls=%async_computation | async-start | bytes 6291456 | tf_op jit(solution)/shard_map/all_to_all | solution.py:48
  93.8 45.2 %all-to-all-start.3 = ((bf16[2,32,32,768]{3,2,0,1:T(8,128)(2,1)}), bf16[2,32,32,768]{3,2,0,1:T(8,128)(2,1)}, u32[]{:S(2)}, u32[]{:S(2)}) async-start(bf16[2,32,32,768]{3,2,0,1:T(8,128)(2,1)} %copy.65), calls=%async_computation.3 | async-start | bytes 6291456 | tf_op jit(solution)/shard_map/all_to_all | solution.py:48
  99.4 2.8 copy-start.5
  99.6 1.7 copy-start.2
  107.5 33.6 %copy-start.7 = (bf16[2,768,768]{2,1,0:T(8,128)(2,1)S(1)}, bf16[2,768,768]{2,1,0:T(8,128)(2,1)}, u32[]{:S(2)}) copy-start(bf16[2,768,768]{2,1,0:T(8,128)(2,1)} %param.11) | copy-start | bytes 7077892
  141.1 6.9 %copy-start.3 = (bf16[2,32,32,768]{3,2,1,0:T(8,128)(2,1)}, bf16[2,32,32,768]{3,2,1,0:T(8,128)(2,1)S(1)}, u32[]{:S(2)}) copy-start(bf16[2,32,32,768]{3,2,1,0:T(8,128)(2,1)S(1)} %copy.66) | copy-start | bytes 9437188
  141.2 6.9 %copy-start.6 = (bf16[2,768,768]{2,1,0:T(8,128)(2,1)S(1)}, bf16[2,768,768]{2,1,0:T(8,128)(2,1)}, u32[]{:S(2)}) copy-start(bf16[2,768,768]{2,1,0:T(8,128)(2,1)} %param.10) | copy-start | bytes 7077892
  148.1 1.6 copy-start.10
  153.1 40.6 %all-to-all-start.4 = ((bf16[4,192,2,1024]{3,1,2,0:T(8,128)(2,1)}), bf16[4,192,2,1024]{3,1,2,0:T(8,128)(2,1)S(1)}, u32[]{:S(2)}, u32[]{:S(2)}) async-start(bf16[4,192,2,1024]{3,1,2,0:T(8,128)(2,1)} %pad_maximum_fusion.1), calls=%async_computation.4 | async-start | bytes 6291456 | tf_op jit(solution)/shard_map/all_to_all | solution.py:63
  156.8 3.4 %copy-start.8 = (bf16[2,768,768]{2,1,0:T(8,128)(2,1)S(1)}, bf16[2,768,768]{2,1,0:T(8,128)(2,1)}, u32[]{:S(2)}) copy-start(bf16[2,768,768]{2,1,0:T(8,128)(2,1)} %param.11) | copy-start | bytes 7077892
  156.8 3.4 %copy-start.9 = (bf16[2,1024,768]{2,1,0:T(8,128)(2,1)S(1)}, bf16[2,1024,768]{2,1,0:T(8,128)(2,1)}, u32[]{:S(2)}) copy-start(bf16[2,1024,768]{2,1,0:T(8,128)(2,1)} %get-tuple-element.8) | copy-start | bytes 9437188
  193.7 1.7 copy-start
  195.4 39.7 %all-to-all-start.1 = ((bf16[4,192,2,1024]{3,1,2,0:T(8,128)(2,1)}), bf16[4,192,2,1024]{3,1,2,0:T(8,128)(2,1)S(1)}, u32[]{:S(2)}, u32[]{:S(2)}) async-start(bf16[4,192,2,1024]{3,1,2,0:T(8,128)(2,1)} %pad_maximum_fusion), calls=%async_computation.1 | async-start | bytes 6291456 | tf_op jit(solution)/shard_map/all_to_all | solution.py:63
  235.1 44.9 %all-to-all-start.5 = ((bf16[192,2,32,32]{0,3,1,2:T(8,128)(2,1)}), bf16[192,2,32,32]{0,3,1,2:T(8,128)(2,1)}, u32[]{:S(2)}, u32[]{:S(2)}) async-start(bf16[192,2,32,32]{0,3,1,2:T(8,128)(2,1)} %copy.71), calls=%async_computation.5 | async-start | bytes 2097152 | tf_op jit(solution)/shard_map/all_to_all | solution.py:66
  280.0 24.4 %all-to-all-start.2 = ((bf16[192,2,32,32]{0,3,1,2:T(8,128)(2,1)}), bf16[192,2,32,32]{0,3,1,2:T(8,128)(2,1)S(1)}, u32[]{:S(2)}, u32[]{:S(2)}) async-start(bf16[192,2,32,32]{0,3,1,2:T(8,128)(2,1)} %copy.59), calls=%async_computation.2 | async-start | bytes 2097152 | tf_op jit(solution)/shard_map/all_to_all | solution.py:66
  287.5 8.4 %copy-start.1 = (pred[512,2,2048]{2,1,0:T(4,128)(4,1)S(1)}, pred[512,2,2048]{2,1,0:T(4,128)(4,1)}, u32[]{:S(2)}) copy-start(pred[512,2,2048]{2,1,0:T(4,128)(4,1)} %eq.58) | copy-start | bytes 6291460
Sparse Core Ops, SparseCore 0:
  10.2 29.4 all-gather.2

commit v3 on v1

--- a/solution.py
+++ b/solution.py
@@ -36,46 +36,56 @@
     token_placer = ((tok_ids == pair[None, :, 0]) | (tok_ids == pair[None, :, 1])).astype(
         jnp.bfloat16
     )
-    weights = gates.reshape(-1)
+    slot_gates = jnp.dot(
+        placer.astype(jnp.float32),
+        gates.reshape(-1),
+        precision=lax.Precision.HIGHEST,
+        preferred_element_type=jnp.float32,
+    )
 
     whole_tokens = lax.all_gather(tokens, "ffn", axis=1, tiled=True)
     whole_cot = lax.all_gather(cotangent, "ffn", axis=1, tiled=True)
 
     def dispatch(send):
-        send = send.astype(jnp.bfloat16).reshape(local_experts, owners, capacity, send.shape[1])
+        send = send.reshape(local_experts, owners, capacity, *send.shape[1:])
         got = lax.all_to_all(send, "expert", split_axis=1, concat_axis=1, tiled=True)
-        return got.reshape(local_experts, slots, got.shape[3])
+        return got.reshape(local_experts, slots, *got.shape[3:])
 
-    rows_in = dispatch(jnp.dot(token_placer, whole_tokens, preferred_element_type=jnp.float32))
-    assigned = (weights[:, None] * jnp.repeat(whole_cot, 2, axis=0).astype(jnp.float32)).astype(
-        jnp.bfloat16
-    )
-    grads_in = dispatch(jnp.dot(placer, assigned, preferred_element_type=jnp.float32))
+    def place(whole):
+        return jnp.dot(token_placer, whole, preferred_element_type=jnp.float32).astype(
+            jnp.bfloat16
+        )
 
-    def send_home(parts):
-        cols = jnp.stack(
-            [
-                lax.psum_scatter(
-                    with_layout_constraint(part, Layout((0, 1))).astype(jnp.bfloat16),
-                    "ffn",
-                    scatter_dimension=0,
-                    tiled=True,
-                )
-                for part in parts
-            ],
-            axis=1,
-        ).astype(jnp.bfloat16)
-        cols = cols.reshape(cols.shape[0], local_experts, owners, capacity)
-        back = lax.all_to_all(cols, "expert", split_axis=2, concat_axis=2, tiled=True)
-        return back.reshape(back.shape[0], rows)
+    rows_in = dispatch(place(whole_tokens))
+    cot_send = place(whole_cot)
 
     preact = jnp.einsum("xsd,xdf->xsf", rows_in, up_weight, preferred_element_type=jnp.float32)
     gating = jax.nn.sigmoid(preact)
     activated = (preact * gating).astype(jnp.bfloat16)
     out_part = [
-        jnp.einsum("fd,sf->ds", down_weight[x], activated[x], preferred_element_type=jnp.float32)
+        with_layout_constraint(
+            jnp.einsum(
+                "fd,sf->ds", down_weight[x], activated[x], preferred_element_type=jnp.float32
+            ),
+            Layout((0, 1)),
+        ).astype(jnp.bfloat16)
         for x in range(local_experts)
     ]
+    out_part, cot_send, slot_gates = lax.optimization_barrier((out_part, cot_send, slot_gates))
+
+    cot_in = dispatch(cot_send)
+    gate_in = dispatch(slot_gates)
+    grads_in = (gate_in[:, :, None] * cot_in.astype(jnp.float32)).astype(jnp.bfloat16)
+
+    def send_home(parts):
+        cols = jnp.stack(
+            [lax.psum_scatter(part, "ffn", scatter_dimension=0, tiled=True) for part in parts],
+            axis=1,
+        )
+        cols = cols.reshape(cols.shape[0], local_experts, owners, capacity)
+        back = lax.all_to_all(cols, "expert", split_axis=2, concat_axis=2, tiled=True)
+        return back.reshape(back.shape[0], rows)
+
     out_home = send_home(out_part)
     back_grad = jnp.einsum(
         "xsd,xfd->xsf", grads_in, down_weight, preferred_element_type=jnp.float32
@@ -88,7 +98,12 @@
         "xsd,xsf->xdf", rows_in, pre_grad, preferred_element_type=jnp.float32
     ).astype(jnp.bfloat16)
     in_part = [
-        jnp.einsum("df,sf->ds", up_weight[x], pre_grad[x], preferred_element_type=jnp.float32)
+        with_layout_constraint(
+            jnp.einsum(
+                "df,sf->ds", up_weight[x], pre_grad[x], preferred_element_type=jnp.float32
+            ),
+            Layout((0, 1)),
+        ).astype(jnp.bfloat16)
         for x in range(local_experts)
     ]
     in_home = send_home(in_part)

time: 286 us -> 255 us (0.89)
  waiting for transfers between devices: 108 us -> 90.3 us
  local copies, waits for them, and re-layouts: 39.9 us -> 29.1 us
    reduce_scatter x4, waiting for transfers between devices: 64.6 us -> 20.7 us  [send_home(): lax.psum_scatter(part, 'ffn', scatter_dimension=0, tiled=True)]
    all_to_all x2 -> x3, waiting for transfers between devices: 37.8 us -> 63.4 us  [dispatch(): lax.all_to_all(send, 'expert', split_axis=1, concat_axis=1, tiled=True)]
    convert_element_type x2 -> x0, local copies, waits for them, and re-layouts: 7.9 us -> none  [shards(): jnp.repeat(whole_cot, 2, axis=0).astype(jnp.float32)]
    all_to_all x2, starting transfers between devices: 17.2 us -> 12.9 us  [send_home(): lax.all_to_all(cols, 'expert', split_axis=2, concat_axis=2, tiled=True)]
    broadcast_in_dim x1 -> x0, local copies, waits for them, and re-layouts: 4.17 us -> none  [shards(): jnp.repeat(whole_cot, 2, axis=0).astype(jnp.float32)]
    all_to_all x2 -> x3, starting transfers between devices: 15.6 us -> 19 us  [dispatch(): lax.all_to_all(send, 'expert', split_axis=1, concat_axis=1, tiled=True)]
    unnamed x24 -> x28, local copies, waits for them, and re-layouts: 5.47 us -> 8.03 us
    dot_general x2 -> x3, matrix products: 8.1 us -> 9.49 us  [the longest x2 5.75 us: place(): jnp.dot(token_placer, whole, preferred_element_type=jnp.float32)]
  transfers between devices with their start and end apart: 8 -> 9, of which waited for: 7 -> 5; matrix products, arithmetic and copies ran while one was open for 26% -> 23% of each run, Pallas kernels for 0% -> 0%
where the time goes in v3:
time: 255 us
  waiting for transfers between devices  90.3 us (35%)
  matrix products  59.4 us (23%)
  starting transfers between devices  32.3 us (13%)
  local copies, waits for them, and re-layouts  29.1 us (11%)
  blocking collectives  25.6 us (10%)
  between operations  14.1 us (6%)
  other arithmetic  3.78 us (1%)
    all_to_all x3, waiting for transfers between devices, dispatch(): lax.all_to_all(send, 'expert', split_axis=1, concat_axis=1, tiled=True)  63.4 us
    reduce_scatter x4, waiting for transfers between devices, send_home(): lax.psum_scatter(part, 'ffn', scatter_dimension=0, tiled=True)  20.7 us
    all_to_all x3, starting transfers between devices, dispatch(): lax.all_to_all(send, 'expert', split_axis=1, concat_axis=1, tiled=True)  19 us
    all_gather x1, blocking collectives, shards(): whole_tokens = lax.all_gather(tokens, 'ffn', axis=1, tiled=True)  12.9 us
    all_to_all x2, starting transfers between devices, send_home(): lax.all_to_all(cols, 'expert', split_axis=2, concat_axis=2, tiled=True)  12.9 us
    all_gather x1, blocking collectives, shards(): whole_cot = lax.all_gather(cotangent, 'ffn', axis=1, tiled=True)  12.8 us
    dot_general x2, matrix products, gather_back(): lax.dot_general(placer, returned, (((0,), (1,)), ((), ())), preferred_ele...  10.7 us
    unnamed x28, local copies, waits for them, and re-layouts  8.03 us
  transfers between devices with their start and end apart: 9, of which 5 were waited for; matrix products, arithmetic and copies ran while one was open for 23% of the time, Pallas kernels for 0%

profile of v3, /device:TPU:1, one launch (start us, length us, event | category | flops | bytes accessed | tf_op | source)
XLA Modules:
  0.0 254.5 jit_solution(3164283209986348818)
XLA Ops:
  10.5 12.9 %all_gather.6 = bf16[512,768]{0,1:T(8,128)(2,1)S(1)} all-gather(bf16[512,192]{0,1:T(8,128)(2,1)S(1)} %copy-done.4), channel_id=1, replica_groups=mesh['expert'=32,'ffn'=4] {'ffn'}, dimensions={1}, use_global_device_ids=true | all-gather | bytes 983040 | tf_op jit(solution)/shard_map/all_gather | solution.py:46
  27.4 10.5 %all-to-all-start = ((bf16[2,32,32,768]{3,2,0,1:T(8,128)(2,1)}), bf16[2,32,32,768]{3,2,0,1:T(8,128)(2,1)S(1)}, u32[]{:S(2)}, u32[]{:S(2)}) async-start(bf16[2,32,32,768]{3,2,0,1:T(8,128)(2,1)} %copy.86), calls=%async_computation | async-start | bytes 6291456 | tf_op jit(solution)/shard_map/all_to_all | solution.py:51
  38.3 3.7 %fusion = f32[1,2048]{1,0:T(1,128)S(1)} fusion(f32[1024,1]{0,1:T(1,128)S(1)} %reshape.157, s32[1024]{0:T(1024)S(1)} %fusion.46), kind=kOutput, calls=%fused_computation.2 | convolution fusion | flops 27262976 | bytes 16384 | tf_op jit(solution)/shard_map/dot_general | solution.py:39
  42.1 12.8 %all_gather.7 = bf16[512,768]{0,1:T(8,128)(2,1)S(1)} all-gather(bf16[512,192]{0,1:T(8,128)(2,1)S(1)} %copy-done.5), channel_id=1, replica_groups=mesh['expert'=32,'ffn'=4] {'ffn'}, dimensions={1}, use_global_device_ids=true | all-gather | bytes 983040 | tf_op jit(solution)/shard_map/all_gather | solution.py:47
  54.8 3.7 %convolution_convert_fusion = bf16[2048,768]{1,0:T(8,128)(2,1)} fusion(bf16[512,768]{0,1:T(8,128)(2,1)S(1)} %all_gather.7, s32[512]{0:T(512)S(1)} %get-tuple-element.13, s32[512]{0:T(512)S(1)} %get-tuple-element.12), kind=kOutput, calls=%fused_computation.14 | convolution fusion | flops 1615331328 | bytes 3936256 | tf_op jit(solution)/shard_map/dot_general | solution.py:55
  58.5 19.1 %all-to-all-done = bf16[2,32,32,768]{3,2,0,1:T(8,128)(2,1)S(1)} async-done(((bf16[2,32,32,768]{3,2,0,1:T(8,128)(2,1)}), bf16[2,32,32,768]{3,2,0,1:T(8,128)(2,1)S(1)}, u32[]{:S(2)}, u32[]{:S(2)}) %all-to-all-start) | async-done | bytes 3145760 | tf_op jit(solution)/shard_map/all_to_all | solution.py:51
  80.4 5.0 %multiply_convert_fusion.1 = (bf16[2,1024,768]{2,1,0:T(8,128)(2,1)S(1)}, f32[2,1024,768]{2,1,0:T(8,128)}) fusion(bf16[2,1024,768]{2,1,0:T(8,128)(2,1)S(1)} %bitcast.62, bf16[2,768,768]{2,1,0:T(8,128)(2,1)S(1)} %copy-done.9), kind=kOutput, calls=%fused_computation.6 | convolution fusion | flops 2423783424 | bytes 14942208 | tf_op jit(solution)/shard_map/xsd,xdf->xsf/dot_general | solution.py:62
  87.1 2.6 %bitcast_convert_fusion.2 = bf16[768,1024]{1,0:T(8,128)(2,1)} fusion(bf16[2,1024,768]{2,1,0:T(8,128)(2,1)S(1)} %get-tuple-element.14, bf16[2,768,768]{2,1,0:T(8,128)(2,1)S(1)} %copy-done.7), kind=kOutput, calls=%fused_computation.18 | convolution fusion | flops 1208745984 | bytes 4325376 | tf_op jit(solution)/shard_map/fd,sf->ds/dot_general | solution.py:67
  89.7 4.5 %bitcast_convert_fusion.3 = bf16[768,1024]{1,0:T(8,128)(2,1)} fusion(bf16[2,1024,768]{2,1,0:T(8,128)(2,1)} %copy-done.11, bf16[2,768,768]{2,1,0:T(8,128)(2,1)} %param.11), kind=kOutput, calls=%fused_computation.19 | convolution fusion | flops 1208745984 | bytes 4325376 | tf_op jit(solution)/shard_map/fd,sf->ds/dot_general | solution.py:67
  94.9 4.4 %all-to-all-start.2 = ((f32[2,32,32]{2,0,1:T(2,128)}), f32[2,32,32]{2,0,1:T(2,128)S(1)}, u32[]{:S(2)}, u32[]{:S(2)}) async-start(f32[2,32,32]{2,0,1:T(2,128)} %copy.95), calls=%async_computation.4 | async-start | bytes 65536 | tf_op jit(solution)/shard_map/all_to_all | solution.py:51
  101.2 5.4 %all-to-all-done.2 = f32[2,32,32]{2,0,1:T(2,128)S(1)} async-done(((f32[2,32,32]{2,0,1:T(2,128)}), f32[2,32,32]{2,0,1:T(2,128)S(1)}, u32[]{:S(2)}, u32[]{:S(2)}) %all-to-all-start.2) | async-done | bytes 8224 | tf_op jit(solution)/shard_map/all_to_all | solution.py:51
  106.6 4.1 %all-to-all-start.3 = ((bf16[2,32,32,768]{3,2,0,1:T(8,128)(2,1)}), bf16[2,32,32,768]{3,2,0,1:T(8,128)(2,1)S(1)}, u32[]{:S(2)}, u32[]{:S(2)}) async-start(bf16[2,32,32,768]{3,2,0,1:T(8,128)(2,1)} %copy.97), calls=%async_computation.5 | async-start | bytes 6291456 | tf_op jit(solution)/shard_map/all_to_all | solution.py:51
  111.6 38.9 %all-to-all-done.3 = bf16[2,32,32,768]{3,2,0,1:T(8,128)(2,1)S(1)} async-done(((bf16[2,32,32,768]{3,2,0,1:T(8,128)(2,1)}), bf16[2,32,32,768]{3,2,0,1:T(8,128)(2,1)S(1)}, u32[]{:S(2)}, u32[]{:S(2)}) %all-to-all-start.3) | async-done | bytes 3145760 | tf_op jit(solution)/shard_map/all_to_all | solution.py:51
  152.5 5.9 %multiply_convert_fusion = bf16[2,1024,768]{2,1,0:T(8,128)(2,1)S(1)} fusion(f32[2,1024,768]{2,1,0:T(8,128)} %get-tuple-element.15, bf16[2,1024,768]{2,1,0:T(8,128)(2,1)S(1)} %fusion.1, bf16[2,768,768]{2,1,0:T(8,128)(2,1)S(1)} %copy-done.8), kind=kOutput, calls=%fused_computation.5 | convolution fusion | flops 2430074880 | bytes 14942208 | tf_op jit(solution)/shard_map/xsd,xfd->xsf/dot_general | solution.py:90
  163.0 4.0 %bitcast_convert_fusion = bf16[768,1024]{1,0:T(8,128)(2,1)} fusion(bf16[2,1024,768]{2,1,0:T(8,128)(2,1)} %copy-done.12, bf16[2,768,768]{2,1,0:T(8,128)(2,1)S(1)} %copy-done.10), kind=kOutput, calls=%fused_computation.16 | convolution fusion | flops 1208745984 | bytes 4325376 | tf_op jit(solution)/shard_map/df,sf->ds/dot_general | solution.py:102
  168.8 7.8 %eq.58 = pred[512,2,2048]{2,1,0:T(4,128)(4,1)} reshape(pred[1024,2048]{1,0:T(8,128)(4,1)S(1)} %iota_compare_fusion.1) | data formatting | bytes 4194304 | tf_op jit(solution)/shard_map/eq | solution.py:33
  180.3 4.3 %all-to-all-start.1 = ((bf16[192,2,32,32]{0,3,1,2:T(8,128)(2,1)}), bf16[192,2,32,32]{0,3,1,2:T(8,128)(2,1)S(1)}, u32[]{:S(2)}, u32[]{:S(2)}) async-start(bf16[192,2,32,32]{0,3,1,2:T(8,128)(2,1)} %copy.91), calls=%async_computation.3 | async-start | bytes 2097152 | tf_op jit(solution)/shard_map/all_to_all | solution.py:86
  184.6 7.0 %convolution_convert_fusion.2 = bf16[2,768,768]{2,1,0:T(8,128)(2,1)} fusion(bf16[2,1024,768]{2,1,0:T(8,128)(2,1)} %copy-done.11, bf16[2,1024,768]{2,1,0:T(8,128)(2,1)} %copy-done.2), kind=kOutput, calls=%fused_computation.28 | convolution fusion | flops 2417098752 | bytes 8650752 | tf_op jit(solution)/shard_map/xsf,xsd->xfd/dot_general | solution.py:94
  192.8 20.7 %reduce-scatter.11.cloned.1.call-done = bf16[192,1024]{1,0:T(8,128)(2,1)} async-done(((bf16[768,1024]{1,0:T(8,128)(2,1)}), bf16[192,1024]{1,0:T(8,128)(2,1)}) %reduce-scatter.11.cloned.1.call-update) | async-done | bytes 393232 | tf_op jit(solution)/shard_map/reduce_scatter | solution.py:82
  216.0 8.5 %all-to-all-start.4 = ((bf16[192,2,32,32]{0,3,1,2:T(8,128)(2,1)}), bf16[192,2,32,32]{0,3,1,2:T(8,128)(2,1)S(1)}, u32[]{:S(2)}, u32[]{:S(2)}) async-start(bf16[192,2,32,32]{0,3,1,2:T(8,128)(2,1)} %copy.101), calls=%async_computation.8 | async-start | bytes 2097152 | tf_op jit(solution)/shard_map/all_to_all | solution.py:86
  224.6 7.1 %convolution_convert_fusion.3 = bf16[2,768,768]{2,1,0:T(8,128)(2,1)} fusion(bf16[2,1024,768]{2,1,0:T(8,128)(2,1)} %bitcast.63, bf16[2,1024,768]{2,1,0:T(8,128)(2,1)} %copy-done.12), kind=kOutput, calls=%fused_computation.29 | convolution fusion | flops 2417098752 | bytes 8650752 | tf_op jit(solution)/shard_map/xsd,xsf->xdf/dot_general | solution.py:97
  231.8 4.3 %fusion.18 = bf16[512,192]{0,1:T(8,128)(2,1)} fusion(bf16[192,2048,1]{0,1,2:T(8,128)(2,1)S(1)} %bitcast.71, pred[512,2,2048]{2,1,0:T(4,128)(4,1)S(1)} %copy-done, f32[512,2]{0,1:T(2,128)S(1)} %copy-done.6), kind=kOutput, calls=%fused_computation.35 | convolution fusion | flops 805601280 | bytes 3084288 | tf_op jit(solution)/shard_map/dot_general | solution.py:112
  236.0 5.4 %all-to-all-done.4 = bf16[192,2,32,32]{0,3,1,2:T(8,128)(2,1)S(1)} async-done(((bf16[192,2,32,32]{0,3,1,2:T(8,128)(2,1)}), bf16[192,2,32,32]{0,3,1,2:T(8,128)(2,1)S(1)}, u32[]{:S(2)}, u32[]{:S(2)}) %all-to-all-start.4) | async-done | bytes 786464 | tf_op jit(solution)/shard_map/all_to_all | solution.py:86
  241.5 6.4 %fusion.21 = bf16[512,192]{0,1:T(8,128)(2,1)} fusion(bf16[192,2048,1]{0,1,2:T(8,128)(2,1)S(1)} %bitcast.70, pred[512,2,2048]{2,1,0:T(4,128)(4,1)} %eq.58), kind=kOutput, calls=%fused_computation.36 | convolution fusion | flops 805404672 | bytes 3080192 | tf_op jit(solution)/shard_map/dot_general | solution.py:112
  (72 shorter events, 31.4 us)
Async XLA Ops:
  7.2 3.4 %copy-start.4 = (bf16[512,192]{0,1:T(8,128)(2,1)S(1)}, bf16[512,192]{0,1:T(8,128)(2,1)}, u32[]{:S(2)}) copy-start(bf16[512,192]{0,1:T(8,128)(2,1)} %param.6) | copy-start | bytes 589828
  27.4 10.6 %copy-start.6 = (f32[512,2]{0,1:T(2,128)S(1)}, f32[512,2]{0,1:T(2,128)}, u32[]{:S(2)}) copy-start(f32[512,2]{0,1:T(2,128)} %param.8) | copy-start | bytes 12292
  27.4 50.2 %all-to-all-start = ((bf16[2,32,32,768]{3,2,0,1:T(8,128)(2,1)}), bf16[2,32,32,768]{3,2,0,1:T(8,128)(2,1)S(1)}, u32[]{:S(2)}, u32[]{:S(2)}) async-start(bf16[2,32,32,768]{3,2,0,1:T(8,128)(2,1)} %copy.86), calls=%async_computation | async-start | bytes 6291456 | tf_op jit(solution)/shard_map/all_to_all | solution.py:51
  37.9 138.7 %reduce-scatter.7.cloned.1.call-start = ((), (), s32[]{:S(2)}) async-start(), calls=%async_computation.10 | async-start | bytes 1966080 | tf_op jit(solution)/shard_map/reduce_scatter | solution.py:82
  38.3 3.8 %copy-start.5 = (bf16[512,192]{0,1:T(8,128)(2,1)S(1)}, bf16[512,192]{0,1:T(8,128)(2,1)}, u32[]{:S(2)}) copy-start(bf16[512,192]{0,1:T(8,128)(2,1)} %param.7) | copy-start | bytes 589828
  77.6 2.8 %copy-start.9 = (bf16[2,768,768]{2,1,0:T(8,128)(2,1)S(1)}, bf16[2,768,768]{2,1,0:T(8,128)(2,1)}, u32[]{:S(2)}) copy-start(bf16[2,768,768]{2,1,0:T(8,128)(2,1)} %param.10) | copy-start | bytes 7077892
  77.9 7.5 %copy-start.1 = (bf16[2,32,32,768]{3,2,1,0:T(8,128)(2,1)}, bf16[2,32,32,768]{3,2,1,0:T(8,128)(2,1)S(1)}, u32[]{:S(2)}) copy-start(bf16[2,32,32,768]{3,2,1,0:T(8,128)(2,1)S(1)} %copy.87) | copy-start | bytes 9437188
  80.4 6.6 %copy-start.7 = (bf16[2,768,768]{2,1,0:T(8,128)(2,1)S(1)}, bf16[2,768,768]{2,1,0:T(8,128)(2,1)}, u32[]{:S(2)}) copy-start(bf16[2,768,768]{2,1,0:T(8,128)(2,1)} %param.11) | copy-start | bytes 7077892
  85.4 1.7 copy-start.11
  89.7 9.6 %copy-start.3 = (bf16[2048,768]{1,0:T(8,128)(2,1)S(1)}, bf16[2048,768]{1,0:T(8,128)(2,1)}, u32[]{:S(2)}) copy-start(bf16[2048,768]{1,0:T(8,128)(2,1)} %convolution_convert_fusion) | copy-start | bytes 9437188
  94.9 11.7 %all-to-all-start.2 = ((f32[2,32,32]{2,0,1:T(2,128)}), f32[2,32,32]{2,0,1:T(2,128)S(1)}, u32[]{:S(2)}, u32[]{:S(2)}) async-start(f32[2,32,32]{2,0,1:T(2,128)} %copy.95), calls=%async_computation.4 | async-start | bytes 65536 | tf_op jit(solution)/shard_map/all_to_all | solution.py:51
  106.6 44.0 %all-to-all-start.3 = ((bf16[2,32,32,768]{3,2,0,1:T(8,128)(2,1)}), bf16[2,32,32,768]{3,2,0,1:T(8,128)(2,1)S(1)}, u32[]{:S(2)}, u32[]{:S(2)}) async-start(bf16[2,32,32,768]{3,2,0,1:T(8,128)(2,1)} %copy.97), calls=%async_computation.5 | async-start | bytes 6291456 | tf_op jit(solution)/shard_map/all_to_all | solution.py:51
  110.7 67.1 %reduce-scatter.5.cloned.1.call-start = ((), (), s32[]{:S(2)}) async-start(), calls=%async_computation.9 | async-start | bytes 1966080 | tf_op jit(solution)/shard_map/reduce_scatter | solution.py:82
  111.5 80.2 %reduce-scatter.9.cloned.1.call-start = ((), (), s32[]{:S(2)}) async-start(), calls=%async_computation.11 | async-start | bytes 1966080 | tf_op jit(solution)/shard_map/reduce_scatter | solution.py:82
  150.8 1.7 copy-start.8
  151.5 7.0 %copy-start.2 = (bf16[2,1024,768]{2,1,0:T(8,128)(2,1)}, bf16[2,1024,768]{2,1,0:T(8,128)(2,1)S(1)}, u32[]{:S(2)}) copy-start(bf16[2,1024,768]{2,1,0:T(8,128)(2,1)S(1)} %fusion.1) | copy-start | bytes 9437188
  152.5 7.6 %copy-start.10 = (bf16[2,768,768]{2,1,0:T(8,128)(2,1)S(1)}, bf16[2,768,768]{2,1,0:T(8,128)(2,1)}, u32[]{:S(2)}) copy-start(bf16[2,768,768]{2,1,0:T(8,128)(2,1)} %param.10) | copy-start | bytes 7077892
  158.4 1.7 copy-start.12
  162.7 50.8 %reduce-scatter.11.cloned.1.call-start = ((), (), s32[]{:S(2)}) async-start(), calls=%async_computation.12 | async-start | bytes 1966080 | tf_op jit(solution)/shard_map/reduce_scatter | solution.py:82
  180.3 35.7 %all-to-all-start.1 = ((bf16[192,2,32,32]{0,3,1,2:T(8,128)(2,1)}), bf16[192,2,32,32]{0,3,1,2:T(8,128)(2,1)S(1)}, u32[]{:S(2)}, u32[]{:S(2)}) async-start(bf16[192,2,32,32]{0,3,1,2:T(8,128)(2,1)} %copy.91), calls=%async_computation.3 | async-start | bytes 2097152 | tf_op jit(solution)/shard_map/all_to_all | solution.py:86
  216.0 25.4 %all-to-all-start.4 = ((bf16[192,2,32,32]{0,3,1,2:T(8,128)(2,1)}), bf16[192,2,32,32]{0,3,1,2:T(8,128)(2,1)S(1)}, u32[]{:S(2)}, u32[]{:S(2)}) async-start(bf16[192,2,32,32]{0,3,1,2:T(8,128)(2,1)} %copy.101), calls=%async_computation.8 | async-start | bytes 2097152 | tf_op jit(solution)/shard_map/all_to_all | solution.py:86
  224.6 7.2 %copy-start = (pred[512,2,2048]{2,1,0:T(4,128)(4,1)S(1)}, pred[512,2,2048]{2,1,0:T(4,128)(4,1)}, u32[]{:S(2)}) copy-start(pred[512,2,2048]{2,1,0:T(4,128)(4,1)} %eq.58) | copy-start | bytes 6291460
Sparse Core Ops, SparseCore 0:
  94.3 22.9 reduce-scatter.6
  120.2 25.3 reduce-scatter.4
  162.9 22.8 reduce-scatter.8
  188.0 25.4 reduce-scatter.10

commit v4 on v3

--- a/solution.py
+++ b/solution.py
@@ -57,7 +57,11 @@
         )
 
     rows_in = dispatch(place(whole_tokens))
-    cot_send = place(whole_cot)
+    scaled = slot_gates[:, None] * jnp.dot(
+        token_placer, whole_cot, preferred_element_type=jnp.float32
+    )
+    rows_in, grads_send = lax.optimization_barrier((rows_in, scaled.astype(jnp.bfloat16)))
+    grads_in = dispatch(grads_send)
 
     preact = jnp.einsum("xsd,xdf->xsf", rows_in, up_weight, preferred_element_type=jnp.float32)
     gating = jax.nn.sigmoid(preact)
@@ -71,11 +75,6 @@
         ).astype(jnp.bfloat16)
         for x in range(local_experts)
     ]
-    out_part, cot_send, slot_gates = lax.optimization_barrier((out_part, cot_send, slot_gates))
-
-    cot_in = dispatch(cot_send)
-    gate_in = dispatch(slot_gates)
-    grads_in = (gate_in[:, :, None] * cot_in.astype(jnp.float32)).astype(jnp.bfloat16)
 
     def send_home(parts):
         cols = jnp.stack(

time: 255 us -> 241 us (0.945)
  waiting for transfers between devices: 90.3 us -> 80.2 us
  starting transfers between devices: 32.3 us -> 28.2 us
    all_to_all x3 -> x2, waiting for transfers between devices: 63.4 us -> 54.1 us  [dispatch(): lax.all_to_all(send, 'expert', split_axis=1, concat_axis=1, tiled=True)]
    all_to_all x3 -> x2, starting transfers between devices: 19 us -> 14.9 us  [dispatch(): lax.all_to_all(send, 'expert', split_axis=1, concat_axis=1, tiled=True)]
    dot_general x0 -> x1, matrix products: none -> 3.86 us  [shards(): jnp.dot(token_placer, whole_cot, preferred_element_type=jnp.float32)]
    dot_general x2 -> x1, matrix products: 5.75 us -> 2.06 us  [place(): jnp.dot(token_placer, whole, preferred_element_type=jnp.float32)]
  transfers between devices with their start and end apart: 9 -> 8, of which waited for: 5 -> 4; matrix products, arithmetic and copies ran while one was open for 23% -> 26% of each run, Pallas kernels for 0% -> 0%
where the time goes in v4:
time: 241 us
  waiting for transfers between devices  80.2 us (33%)
  matrix products  59.6 us (25%)
  local copies, waits for them, and re-layouts  29.7 us (12%)
  starting transfers between devices  28.2 us (12%)
  blocking collectives  25.6 us (11%)
  between operations  14 us (6%)
  other arithmetic  3.13 us (1%)
    all_to_all x2, waiting for transfers between devices, dispatch(): lax.all_to_all(send, 'expert', split_axis=1, concat_axis=1, tiled=True)  54.1 us
    reduce_scatter x4, waiting for transfers between devices, send_home(): lax.psum_scatter(part, 'ffn', scatter_dimension=0, tiled=True)  20.6 us
    all_to_all x2, starting transfers between devices, dispatch(): lax.all_to_all(send, 'expert', split_axis=1, concat_axis=1, tiled=True)  14.9 us
    all_to_all x2, starting transfers between devices, send_home(): lax.all_to_all(cols, 'expert', split_axis=2, concat_axis=2, tiled=True)  12.9 us
    all_gather x1, blocking collectives, shards(): whole_tokens = lax.all_gather(tokens, 'ffn', axis=1, tiled=True)  12.9 us
    all_gather x1, blocking collectives, shards(): whole_cot = lax.all_gather(cotangent, 'ffn', axis=1, tiled=True)  12.8 us
    dot_general x2, matrix products, gather_back(): lax.dot_general(placer, returned, (((0,), (1,)), ((), ())), preferred_ele...  10.7 us
    unnamed x28, local copies, waits for them, and re-layouts  9.39 us
  transfers between devices with their start and end apart: 8, of which 4 were waited for; matrix products, arithmetic and copies ran while one was open for 26% of the time, Pallas kernels for 0%

profile of v4, /device:TPU:1, one launch (start us, length us, event | category | flops | bytes accessed | tf_op | source)
XLA Modules:
  0.0 240.6 jit_solution(4004977149829489381)
XLA Ops:
  10.5 12.9 %all_gather.6 = bf16[512,768]{0,1:T(8,128)(2,1)S(1)} all-gather(bf16[512,192]{0,1:T(8,128)(2,1)S(1)} %copy-done.4), channel_id=1, replica_groups=mesh['expert'=32,'ffn'=4] {'ffn'}, dimensions={1}, use_global_device_ids=true | all-gather | bytes 983040 | tf_op jit(solution)/shard_map/all_gather | solution.py:46
  27.4 10.5 %all-to-all-start = ((bf16[2,32,32,768]{3,2,0,1:T(8,128)(2,1)}), bf16[2,32,32,768]{3,2,0,1:T(8,128)(2,1)S(1)}, u32[]{:S(2)}, u32[]{:S(2)}) async-start(bf16[2,32,32,768]{3,2,0,1:T(8,128)(2,1)} %copy.61), calls=%async_computation | async-start | bytes 6291456 | tf_op jit(solution)/shard_map/all_to_all | solution.py:51
  38.3 3.7 %fusion = f32[1,2048]{1,0:T(1,128)S(1)} fusion(f32[1024,1]{0,1:T(1,128)S(1)} %reshape.153, s32[1024]{0:T(1024)S(1)} %fusion.45), kind=kOutput, calls=%fused_computation.2 | convolution fusion | flops 27262976 | bytes 16384 | tf_op jit(solution)/shard_map/dot_general | solution.py:39
  42.1 12.8 %all_gather.7 = bf16[512,768]{0,1:T(8,128)(2,1)S(1)} all-gather(bf16[512,192]{0,1:T(8,128)(2,1)S(1)} %copy-done.5), channel_id=1, replica_groups=mesh['expert'=32,'ffn'=4] {'ffn'}, dimensions={1}, use_global_device_ids=true | all-gather | bytes 983040 | tf_op jit(solution)/shard_map/all_gather | solution.py:47
  54.8 3.9 %multiply_convert_fusion.2 = bf16[2048,768]{1,0:T(8,128)(2,1)} fusion(bf16[512,768]{0,1:T(8,128)(2,1)S(1)} %all_gather.7, f32[2048]{0:T(1024)S(1)} %bitcast.72, s32[512]{0:T(512)S(1)} %get-tuple-element.9, s32[512]{0:T(512)S(1)} %get-tuple-element.8), kind=kOutput, calls=%fused_computation.6 | convolution fusion | flops 1616904192 | bytes 3944448 | tf_op jit(solution)/shard_map/dot_general | solution.py:60
  58.7 18.9 %all-to-all-done = bf16[2,32,32,768]{3,2,0,1:T(8,128)(2,1)S(1)} async-done(((bf16[2,32,32,768]{3,2,0,1:T(8,128)(2,1)}), bf16[2,32,32,768]{3,2,0,1:T(8,128)(2,1)S(1)}, u32[]{:S(2)}, u32[]{:S(2)}) %all-to-all-start) | async-done | bytes 3145760 | tf_op jit(solution)/shard_map/all_to_all | solution.py:51
  80.4 4.9 %multiply_convert_fusion.1 = (bf16[2,1024,768]{2,1,0:T(8,128)(2,1)S(1)}, f32[2,1024,768]{2,1,0:T(8,128)}) fusion(bf16[2,1024,768]{2,1,0:T(8,128)(2,1)S(1)} %bitcast.60, bf16[2,768,768]{2,1,0:T(8,128)(2,1)S(1)} %copy-done.9), kind=kOutput, calls=%fused_computation.4 | convolution fusion | flops 2423783424 | bytes 14942208 | tf_op jit(solution)/shard_map/xsd,xdf->xsf/dot_general | solution.py:66
  87.0 2.6 %bitcast_convert_fusion.2 = bf16[768,1024]{1,0:T(8,128)(2,1)} fusion(bf16[2,1024,768]{2,1,0:T(8,128)(2,1)S(1)} %get-tuple-element.10, bf16[2,768,768]{2,1,0:T(8,128)(2,1)S(1)} %copy-done.7), kind=kOutput, calls=%fused_computation.16 | convolution fusion | flops 1208745984 | bytes 4325376 | tf_op jit(solution)/shard_map/fd,sf->ds/dot_general | solution.py:71
  91.6 4.4 %all-to-all-start.2 = ((bf16[2,32,32,768]{3,2,0,1:T(8,128)(2,1)}), bf16[2,32,32,768]{3,2,0,1:T(8,128)(2,1)S(1)}, u32[]{:S(2)}, u32[]{:S(2)}) async-start(bf16[2,32,32,768]{3,2,0,1:T(8,128)(2,1)} %copy.70), calls=%async_computation.4 | async-start | bytes 6291456 | tf_op jit(solution)/shard_map/all_to_all | solution.py:51
  96.1 4.6 %bitcast_convert_fusion.3 = bf16[768,1024]{1,0:T(8,128)(2,1)} fusion(bf16[2,1024,768]{2,1,0:T(8,128)(2,1)} %copy-done.11, bf16[2,768,768]{2,1,0:T(8,128)(2,1)} %param.11), kind=kOutput, calls=%fused_computation.17 | convolution fusion | flops 1208745984 | bytes 4325376 | tf_op jit(solution)/shard_map/fd,sf->ds/dot_general | solution.py:71
  100.7 35.1 %all-to-all-done.2 = bf16[2,32,32,768]{3,2,0,1:T(8,128)(2,1)S(1)} async-done(((bf16[2,32,32,768]{3,2,0,1:T(8,128)(2,1)}), bf16[2,32,32,768]{3,2,0,1:T(8,128)(2,1)S(1)}, u32[]{:S(2)}, u32[]{:S(2)}) %all-to-all-start.2) | async-done | bytes 3145760 | tf_op jit(solution)/shard_map/all_to_all | solution.py:51
  136.1 2.6 %copy-done.8 = bf16[2,768,768]{2,1,0:T(8,128)(2,1)S(1)} copy-done((bf16[2,768,768]{2,1,0:T(8,128)(2,1)S(1)}, bf16[2,768,768]{2,1,0:T(8,128)(2,1)}, u32[]{:S(2)}) %copy-start.8) | copy-done | bytes 2359320
  138.7 5.9 %multiply_convert_fusion = bf16[2,1024,768]{2,1,0:T(8,128)(2,1)S(1)} fusion(f32[2,1024,768]{2,1,0:T(8,128)} %get-tuple-element.11, bf16[2,1024,768]{2,1,0:T(8,128)(2,1)S(1)} %bitcast.62, bf16[2,768,768]{2,1,0:T(8,128)(2,1)S(1)} %copy-done.8), kind=kOutput, calls=%fused_computation.3 | convolution fusion | flops 2430074880 | bytes 14942208 | tf_op jit(solution)/shard_map/xsd,xfd->xsf/dot_general | solution.py:89
  146.2 2.6 %bitcast_convert_fusion.1 = bf16[768,1024]{1,0:T(8,128)(2,1)} fusion(bf16[2,1024,768]{2,1,0:T(8,128)(2,1)S(1)} %multiply_convert_fusion, bf16[2,768,768]{2,1,0:T(8,128)(2,1)S(1)} %copy-done.10), kind=kOutput, calls=%fused_computation.15 | convolution fusion | flops 1208745984 | bytes 4325376 | tf_op jit(solution)/shard_map/df,sf->ds/dot_general | solution.py:101
  149.1 4.0 %bitcast_convert_fusion = bf16[768,1024]{1,0:T(8,128)(2,1)} fusion(bf16[2,1024,768]{2,1,0:T(8,128)(2,1)} %copy-done.12, bf16[2,768,768]{2,1,0:T(8,128)(2,1)S(1)} %copy-done.10), kind=kOutput, calls=%fused_computation.14 | convolution fusion | flops 1208745984 | bytes 4325376 | tf_op jit(solution)/shard_map/df,sf->ds/dot_general | solution.py:101
  154.9 7.8 %eq.58 = pred[512,2,2048]{2,1,0:T(4,128)(4,1)} reshape(pred[1024,2048]{1,0:T(8,128)(4,1)S(1)} %iota_compare_fusion.1) | data formatting | bytes 4194304 | tf_op jit(solution)/shard_map/eq | solution.py:33
  166.4 4.3 %all-to-all-start.1 = ((bf16[192,2,32,32]{0,3,1,2:T(8,128)(2,1)}), bf16[192,2,32,32]{0,3,1,2:T(8,128)(2,1)S(1)}, u32[]{:S(2)}, u32[]{:S(2)}) async-start(bf16[192,2,32,32]{0,3,1,2:T(8,128)(2,1)} %copy.66), calls=%async_computation.3 | async-start | bytes 2097152 | tf_op jit(solution)/shard_map/all_to_all | solution.py:85
  170.7 7.0 %convolution_convert_fusion.2 = bf16[2,768,768]{2,1,0:T(8,128)(2,1)} fusion(bf16[2,1024,768]{2,1,0:T(8,128)(2,1)} %bitcast.61, bf16[2,1024,768]{2,1,0:T(8,128)(2,1)} %copy-done.12), kind=kOutput, calls=%fused_computation.27 | convolution fusion | flops 2417098752 | bytes 8650752 | tf_op jit(solution)/shard_map/xsd,xsf->xdf/dot_general | solution.py:96
  178.9 20.6 %reduce-scatter.11.cloned.1.call-done = bf16[192,1024]{1,0:T(8,128)(2,1)} async-done(((bf16[768,1024]{1,0:T(8,128)(2,1)}), bf16[192,1024]{1,0:T(8,128)(2,1)}) %reduce-scatter.11.cloned.1.call-update) | async-done | bytes 393232 | tf_op jit(solution)/shard_map/reduce_scatter | solution.py:81
  202.0 8.6 %all-to-all-start.3 = ((bf16[192,2,32,32]{0,3,1,2:T(8,128)(2,1)}), bf16[192,2,32,32]{0,3,1,2:T(8,128)(2,1)S(1)}, u32[]{:S(2)}, u32[]{:S(2)}) async-start(bf16[192,2,32,32]{0,3,1,2:T(8,128)(2,1)} %copy.74), calls=%async_computation.7 | async-start | bytes 2097152 | tf_op jit(solution)/shard_map/all_to_all | solution.py:85
  210.6 7.1 %convolution_convert_fusion.1 = bf16[2,768,768]{2,1,0:T(8,128)(2,1)} fusion(bf16[2,1024,768]{2,1,0:T(8,128)(2,1)} %copy-done.11, bf16[2,1024,768]{2,1,0:T(8,128)(2,1)} %bitcast.63), kind=kOutput, calls=%fused_computation.26 | convolution fusion | flops 2417098752 | bytes 8650752 | tf_op jit(solution)/shard_map/xsf,xsd->xfd/dot_general | solution.py:93
  217.8 4.3 %fusion.17 = bf16[512,192]{0,1:T(8,128)(2,1)} fusion(bf16[192,2048,1]{0,1,2:T(8,128)(2,1)S(1)} %bitcast.71, pred[512,2,2048]{2,1,0:T(4,128)(4,1)S(1)} %copy-done, f32[512,2]{0,1:T(2,128)S(1)} %copy-done.6), kind=kOutput, calls=%fused_computation.33 | convolution fusion | flops 805601280 | bytes 3084288 | tf_op jit(solution)/shard_map/dot_general | solution.py:111
  222.1 5.4 %all-to-all-done.3 = bf16[192,2,32,32]{0,3,1,2:T(8,128)(2,1)S(1)} async-done(((bf16[192,2,32,32]{0,3,1,2:T(8,128)(2,1)}), bf16[192,2,32,32]{0,3,1,2:T(8,128)(2,1)S(1)}, u32[]{:S(2)}, u32[]{:S(2)}) %all-to-all-start.3) | async-done | bytes 786464 | tf_op jit(solution)/shard_map/all_to_all | solution.py:85
  227.6 6.4 %fusion.20 = bf16[512,192]{0,1:T(8,128)(2,1)} fusion(bf16[192,2048,1]{0,1,2:T(8,128)(2,1)S(1)} %bitcast.70, pred[512,2,2048]{2,1,0:T(4,128)(4,1)} %eq.58), kind=kOutput, calls=%fused_computation.34 | convolution fusion | flops 805404672 | bytes 3080192 | tf_op jit(solution)/shard_map/dot_general | solution.py:111
  (65 shorter events, 25.6 us)
Async XLA Ops:
  7.2 3.4 %copy-start.4 = (bf16[512,192]{0,1:T(8,128)(2,1)S(1)}, bf16[512,192]{0,1:T(8,128)(2,1)}, u32[]{:S(2)}) copy-start(bf16[512,192]{0,1:T(8,128)(2,1)} %param.6) | copy-start | bytes 589828
  27.4 10.6 %copy-start.6 = (f32[512,2]{0,1:T(2,128)S(1)}, f32[512,2]{0,1:T(2,128)}, u32[]{:S(2)}) copy-start(f32[512,2]{0,1:T(2,128)} %param.8) | copy-start | bytes 12292
  27.4 50.2 %all-to-all-start = ((bf16[2,32,32,768]{3,2,0,1:T(8,128)(2,1)}), bf16[2,32,32,768]{3,2,0,1:T(8,128)(2,1)S(1)}, u32[]{:S(2)}, u32[]{:S(2)}) async-start(bf16[2,32,32,768]{3,2,0,1:T(8,128)(2,1)} %copy.61), calls=%async_computation | async-start | bytes 6291456 | tf_op jit(solution)/shard_map/all_to_all | solution.py:51
  37.9 124.7 %reduce-scatter.7.cloned.1.call-start = ((), (), s32[]{:S(2)}) async-start(), calls=%async_computation.9 | async-start | bytes 1966080 | tf_op jit(solution)/shard_map/reduce_scatter | solution.py:81
  38.3 3.8 %copy-start.5 = (bf16[512,192]{0,1:T(8,128)(2,1)S(1)}, bf16[512,192]{0,1:T(8,128)(2,1)}, u32[]{:S(2)}) copy-start(bf16[512,192]{0,1:T(8,128)(2,1)} %param.7) | copy-start | bytes 589828
  77.7 2.8 %copy-start.9 = (bf16[2,768,768]{2,1,0:T(8,128)(2,1)S(1)}, bf16[2,768,768]{2,1,0:T(8,128)(2,1)}, u32[]{:S(2)}) copy-start(bf16[2,768,768]{2,1,0:T(8,128)(2,1)} %param.10) | copy-start | bytes 7077892
  77.9 7.5 %copy-start.1 = (bf16[2,32,32,768]{3,2,1,0:T(8,128)(2,1)}, bf16[2,32,32,768]{3,2,1,0:T(8,128)(2,1)S(1)}, u32[]{:S(2)}) copy-start(bf16[2,32,32,768]{3,2,1,0:T(8,128)(2,1)S(1)} %copy.62) | copy-start | bytes 9437188
  80.4 6.6 %copy-start.7 = (bf16[2,768,768]{2,1,0:T(8,128)(2,1)S(1)}, bf16[2,768,768]{2,1,0:T(8,128)(2,1)}, u32[]{:S(2)}) copy-start(bf16[2,768,768]{2,1,0:T(8,128)(2,1)} %param.11) | copy-start | bytes 7077892
  85.4 1.6 copy-start.11
  87.0 2.6 %copy-start.3 = (bf16[2048,768]{1,0:T(8,128)(2,1)S(1)}, bf16[2048,768]{1,0:T(8,128)(2,1)}, u32[]{:S(2)}) copy-start(bf16[2048,768]{1,0:T(8,128)(2,1)} %multiply_convert_fusion.2) | copy-start | bytes 9437188
  91.6 44.2 %all-to-all-start.2 = ((bf16[2,32,32,768]{3,2,0,1:T(8,128)(2,1)}), bf16[2,32,32,768]{3,2,0,1:T(8,128)(2,1)S(1)}, u32[]{:S(2)}, u32[]{:S(2)}) async-start(bf16[2,32,32,768]{3,2,0,1:T(8,128)(2,1)} %copy.70), calls=%async_computation.4 | async-start | bytes 6291456 | tf_op jit(solution)/shard_map/all_to_all | solution.py:51
  96.1 67.8 %reduce-scatter.5.cloned.1.call-start = ((), (), s32[]{:S(2)}) async-start(), calls=%async_computation.8 | async-start | bytes 1966080 | tf_op jit(solution)/shard_map/reduce_scatter | solution.py:81
  100.7 77.0 %reduce-scatter.9.cloned.1.call-start = ((), (), s32[]{:S(2)}) async-start(), calls=%async_computation.10 | async-start | bytes 1966080 | tf_op jit(solution)/shard_map/reduce_scatter | solution.py:81
  135.9 2.8 %copy-start.8 = (bf16[2,768,768]{2,1,0:T(8,128)(2,1)S(1)}, bf16[2,768,768]{2,1,0:T(8,128)(2,1)}, u32[]{:S(2)}) copy-start(bf16[2,768,768]{2,1,0:T(8,128)(2,1)} %param.11) | copy-start | bytes 7077892
  136.1 8.5 %copy-start.2 = (bf16[2,32,32,768]{3,2,1,0:T(8,128)(2,1)}, bf16[2,32,32,768]{3,2,1,0:T(8,128)(2,1)S(1)}, u32[]{:S(2)}) copy-start(bf16[2,32,32,768]{3,2,1,0:T(8,128)(2,1)S(1)} %copy.71) | copy-start | bytes 9437188
  138.7 7.5 %copy-start.10 = (bf16[2,768,768]{2,1,0:T(8,128)(2,1)S(1)}, bf16[2,768,768]{2,1,0:T(8,128)(2,1)}, u32[]{:S(2)}) copy-start(bf16[2,768,768]{2,1,0:T(8,128)(2,1)} %param.10) | copy-start | bytes 7077892
  144.6 1.6 copy-start.12
  148.8 50.7 %reduce-scatter.11.cloned.1.call-start = ((), (), s32[]{:S(2)}) async-start(), calls=%async_computation.11 | async-start | bytes 1966080 | tf_op jit(solution)/shard_map/reduce_scatter | solution.py:81
  166.4 35.7 %all-to-all-start.1 = ((bf16[192,2,32,32]{0,3,1,2:T(8,128)(2,1)}), bf16[192,2,32,32]{0,3,1,2:T(8,128)(2,1)S(1)}, u32[]{:S(2)}, u32[]{:S(2)}) async-start(bf16[192,2,32,32]{0,3,1,2:T(8,128)(2,1)} %copy.66), calls=%async_computation.3 | async-start | bytes 2097152 | tf_op jit(solution)/shard_map/all_to_all | solution.py:85
  202.0 25.5 %all-to-all-start.3 = ((bf16[192,2,32,32]{0,3,1,2:T(8,128)(2,1)}), bf16[192,2,32,32]{0,3,1,2:T(8,128)(2,1)S(1)}, u32[]{:S(2)}, u32[]{:S(2)}) async-start(bf16[192,2,32,32]{0,3,1,2:T(8,128)(2,1)} %copy.74), calls=%async_computation.7 | async-start | bytes 2097152 | tf_op jit(solution)/shard_map/all_to_all | solution.py:85
  210.6 7.2 %copy-start = (pred[512,2,2048]{2,1,0:T(4,128)(4,1)S(1)}, pred[512,2,2048]{2,1,0:T(4,128)(4,1)}, u32[]{:S(2)}) copy-start(pred[512,2,2048]{2,1,0:T(4,128)(4,1)} %eq.58) | copy-start | bytes 6291460
Sparse Core Ops, SparseCore 0:
  89.8 22.9 reduce-scatter.6
  115.7 25.3 reduce-scatter.4
  148.9 22.8 reduce-scatter.8
  174.1 25.3 reduce-scatter.10

commit v5 on v4

--- a/solution.py
+++ b/solution.py
@@ -76,16 +76,24 @@
         for x in range(local_experts)
     ]
 
-    def send_home(parts):
+    def reduce_cols(part, on_sparse_core):
+        if on_sparse_core:
+            return lax.psum_scatter(part, "ffn", scatter_dimension=0, tiled=True)
+        ffn = lax.axis_size("ffn")
+        pieces = part.reshape(ffn, part.shape[0] // ffn, part.shape[1])
+        pieces = lax.all_to_all(pieces, "ffn", split_axis=0, concat_axis=0, tiled=True)
+        return jnp.sum(pieces.astype(jnp.float32), axis=0).astype(jnp.bfloat16)
+
+    def send_home(parts, spread):
         cols = jnp.stack(
-            [lax.psum_scatter(part, "ffn", scatter_dimension=0, tiled=True) for part in parts],
+            [reduce_cols(part, not spread or x % 2 == 0) for x, part in enumerate(parts)],
             axis=1,
         )
         cols = cols.reshape(cols.shape[0], local_experts, owners, capacity)
         back = lax.all_to_all(cols, "expert", split_axis=2, concat_axis=2, tiled=True)
         return back.reshape(back.shape[0], rows)
 
-    out_home = send_home(out_part)
+    out_home = send_home(out_part, False)
     back_grad = jnp.einsum(
         "xsd,xfd->xsf", grads_in, down_weight, preferred_element_type=jnp.float32
     )
@@ -105,7 +113,7 @@
         ).astype(jnp.bfloat16)
         for x in range(local_experts)
     ]
-    in_home = send_home(in_part)
+    in_home = send_home(in_part, True)
 
     def gather_back(returned):
         picked = lax.dot_general(

time: 241 us -> 247 us (1.025)
  waiting for transfers between devices: 80.2 us -> 82.9 us
    reduce_scatter x4 -> x3, waiting for transfers between devices: 20.6 us -> 0.04 us  [reduce_cols(): return lax.psum_scatter(part, 'ffn', scatter_dimension=0, tiled=True)]
    all_to_all x0 -> x1, waiting for transfers between devices: none -> 17.9 us  [reduce_cols(): lax.all_to_all(pieces, 'ffn', split_axis=0, concat_axis=0, tiled=True)]
    all_to_all x2, waiting for transfers between devices: 5.43 us -> 10.9 us  [send_home(): lax.all_to_all(cols, 'expert', split_axis=2, concat_axis=2, tiled=True)]
    all_to_all x0 -> x1, starting transfers between devices: none -> 4.57 us  [reduce_cols(): lax.all_to_all(pieces, 'ffn', split_axis=0, concat_axis=0, tiled=True)]
    all_to_all x2, starting transfers between devices: 12.9 us -> 10.4 us  [send_home(): lax.all_to_all(cols, 'expert', split_axis=2, concat_axis=2, tiled=True)]
  transfers between devices with their start and end apart: 8 -> 8, of which waited for: 4 -> 5; matrix products, arithmetic and copies ran while one was open for 26% -> 26% of each run, Pallas kernels for 0% -> 0%
where the time goes in v5:
time: 247 us; the launch traced here: 246 us
  waiting for transfers between devices  82.9 us (34%)
  matrix products  59.7 us (24%)
  starting transfers between devices  30 us (12%)
  local copies, waits for them, and re-layouts  28.7 us (12%)
  blocking collectives  25.6 us (10%)
  between operations  14 us (6%)
  other arithmetic  4.85 us (2%)
    all_to_all x2, waiting for transfers between devices, dispatch(): lax.all_to_all(send, 'expert', split_axis=1, concat_axis=1, tiled=True)  54.1 us
    all_to_all x1, waiting for transfers between devices, reduce_cols(): lax.all_to_all(pieces, 'ffn', split_axis=0, concat_axis=0, tiled=True)  17.9 us
    all_to_all x2, starting transfers between devices, dispatch(): lax.all_to_all(send, 'expert', split_axis=1, concat_axis=1, tiled=True)  14.9 us
    all_gather x1, blocking collectives, shards(): whole_tokens = lax.all_gather(tokens, 'ffn', axis=1, tiled=True)  12.9 us
    all_gather x1, blocking collectives, shards(): whole_cot = lax.all_gather(cotangent, 'ffn', axis=1, tiled=True)  12.8 us
    all_to_all x2, waiting for transfers between devices, send_home(): lax.all_to_all(cols, 'expert', split_axis=2, concat_axis=2, tiled=True)  10.9 us
    dot_general x2, matrix products, gather_back(): lax.dot_general(placer, returned, (((0,), (1,)), ((), ())), preferred_ele...  10.7 us
    all_to_all x2, starting transfers between devices, send_home(): lax.all_to_all(cols, 'expert', split_axis=2, concat_axis=2, tiled=True)  10.4 us
  transfers between devices with their start and end apart: 8, of which 5 were waited for; matrix products, arithmetic and copies ran while one was open for 26% of the time, Pallas kernels for 0%

profile of v5, /device:TPU:1, one launch (start us, length us, event | category | flops | bytes accessed | tf_op | source)
XLA Modules:
  0.0 245.8 jit_solution(6722378638710623595)
XLA Ops:
  10.5 12.9 %all_gather.6 = bf16[512,768]{0,1:T(8,128)(2,1)S(1)} all-gather(bf16[512,192]{0,1:T(8,128)(2,1)S(1)} %copy-done.4), channel_id=1, replica_groups=mesh['expert'=32,'ffn'=4] {'ffn'}, dimensions={1}, use_global_device_ids=true | all-gather | bytes 983040 | tf_op jit(solution)/shard_map/all_gather | solution.py:46
  27.4 10.5 %all-to-all-start = ((bf16[2,32,32,768]{3,2,0,1:T(8,128)(2,1)}), bf16[2,32,32,768]{3,2,0,1:T(8,128)(2,1)S(1)}, u32[]{:S(2)}, u32[]{:S(2)}) async-start(bf16[2,32,32,768]{3,2,0,1:T(8,128)(2,1)} %copy.59), calls=%async_computation | async-start | bytes 6291456 | tf_op jit(solution)/shard_map/all_to_all | solution.py:51
  38.3 3.7 %fusion = f32[1,2048]{1,0:T(1,128)S(1)} fusion(f32[1024,1]{0,1:T(1,128)S(1)} %reshape.157, s32[1024]{0:T(1024)S(1)} %fusion.45), kind=kOutput, calls=%fused_computation.2 | convolution fusion | flops 27262976 | bytes 16384 | tf_op jit(solution)/shard_map/dot_general | solution.py:39
  42.1 12.8 %all_gather.7 = bf16[512,768]{0,1:T(8,128)(2,1)S(1)} all-gather(bf16[512,192]{0,1:T(8,128)(2,1)S(1)} %copy-done.5), channel_id=1, replica_groups=mesh['expert'=32,'ffn'=4] {'ffn'}, dimensions={1}, use_global_device_ids=true | all-gather | bytes 983040 | tf_op jit(solution)/shard_map/all_gather | solution.py:47
  54.8 3.8 %multiply_convert_fusion.2 = bf16[2048,768]{1,0:T(8,128)(2,1)} fusion(bf16[512,768]{0,1:T(8,128)(2,1)S(1)} %all_gather.7, f32[2048]{0:T(1024)S(1)} %bitcast.73, s32[512]{0:T(512)S(1)} %get-tuple-element.9, s32[512]{0:T(512)S(1)} %get-tuple-element.8), kind=kOutput, calls=%fused_computation.6 | convolution fusion | flops 1616904192 | bytes 3944448 | tf_op jit(solution)/shard_map/dot_general | solution.py:60
  58.7 19.0 %all-to-all-done = bf16[2,32,32,768]{3,2,0,1:T(8,128)(2,1)S(1)} async-done(((bf16[2,32,32,768]{3,2,0,1:T(8,128)(2,1)}), bf16[2,32,32,768]{3,2,0,1:T(8,128)(2,1)S(1)}, u32[]{:S(2)}, u32[]{:S(2)}) %all-to-all-start) | async-done | bytes 3145760 | tf_op jit(solution)/shard_map/all_to_all | solution.py:51
  80.4 5.0 %multiply_convert_fusion.1 = (bf16[2,1024,768]{2,1,0:T(8,128)(2,1)S(1)}, f32[2,1024,768]{2,1,0:T(8,128)}) fusion(bf16[2,1024,768]{2,1,0:T(8,128)(2,1)S(1)} %bitcast.61, bf16[2,768,768]{2,1,0:T(8,128)(2,1)S(1)} %copy-done.9), kind=kOutput, calls=%fused_computation.4 | convolution fusion | flops 2423783424 | bytes 14942208 | tf_op jit(solution)/shard_map/xsd,xdf->xsf/dot_general | solution.py:66
  87.1 2.6 %bitcast_convert_fusion.2 = bf16[768,1024]{1,0:T(8,128)(2,1)} fusion(bf16[2,1024,768]{2,1,0:T(8,128)(2,1)S(1)} %get-tuple-element.10, bf16[2,768,768]{2,1,0:T(8,128)(2,1)S(1)} %copy-done.7), kind=kOutput, calls=%fused_computation.16 | convolution fusion | flops 1208745984 | bytes 4325376 | tf_op jit(solution)/shard_map/fd,sf->ds/dot_general | solution.py:71
  91.7 4.4 %all-to-all-start.2 = ((bf16[2,32,32,768]{3,2,0,1:T(8,128)(2,1)}), bf16[2,32,32,768]{3,2,0,1:T(8,128)(2,1)S(1)}, u32[]{:S(2)}, u32[]{:S(2)}) async-start(bf16[2,32,32,768]{3,2,0,1:T(8,128)(2,1)} %copy.68), calls=%async_computation.4 | async-start | bytes 6291456 | tf_op jit(solution)/shard_map/all_to_all | solution.py:51
  96.2 4.6 %bitcast_convert_fusion.3 = bf16[768,1024]{1,0:T(8,128)(2,1)} fusion(bf16[2,1024,768]{2,1,0:T(8,128)(2,1)} %copy-done.11, bf16[2,768,768]{2,1,0:T(8,128)(2,1)} %param.11), kind=kOutput, calls=%fused_computation.17 | convolution fusion | flops 1208745984 | bytes 4325376 | tf_op jit(solution)/shard_map/fd,sf->ds/dot_general | solution.py:71
  100.8 35.1 %all-to-all-done.2 = bf16[2,32,32,768]{3,2,0,1:T(8,128)(2,1)S(1)} async-done(((bf16[2,32,32,768]{3,2,0,1:T(8,128)(2,1)}), bf16[2,32,32,768]{3,2,0,1:T(8,128)(2,1)S(1)}, u32[]{:S(2)}, u32[]{:S(2)}) %all-to-all-start.2) | async-done | bytes 3145760 | tf_op jit(solution)/shard_map/all_to_all | solution.py:51
  138.8 5.9 %multiply_convert_fusion = bf16[2,1024,768]{2,1,0:T(8,128)(2,1)S(1)} fusion(f32[2,1024,768]{2,1,0:T(8,128)} %get-tuple-element.11, bf16[2,1024,768]{2,1,0:T(8,128)(2,1)S(1)} %bitcast.63, bf16[2,768,768]{2,1,0:T(8,128)(2,1)S(1)} %copy-done.8), kind=kOutput, calls=%fused_computation.3 | convolution fusion | flops 2430074880 | bytes 14942208 | tf_op jit(solution)/shard_map/xsd,xfd->xsf/dot_general | solution.py:97
  148.9 4.0 %bitcast_convert_fusion = bf16[768,1024]{1,0:T(8,128)(2,1)} fusion(bf16[2,1024,768]{2,1,0:T(8,128)(2,1)} %copy-done.12, bf16[2,768,768]{2,1,0:T(8,128)(2,1)S(1)} %copy-done.10), kind=kOutput, calls=%fused_computation.14 | convolution fusion | flops 1208745984 | bytes 4325376 | tf_op jit(solution)/shard_map/df,sf->ds/dot_general | solution.py:109
  152.9 4.6 %all-to-all-start.3 = ((bf16[4,192,1024]{2,1,0:T(8,128)(2,1)}), bf16[4,192,1024]{2,1,0:T(8,128)(2,1)}, u32[]{:S(2)}, u32[]{:S(2)}) async-start(bf16[4,192,1024]{2,1,0:T(8,128)(2,1)} %bitcast.22), calls=%async_computation.6 | async-start | bytes 3145728 | tf_op jit(solution)/shard_map/all_to_all | solution.py:84
  159.2 7.8 %eq.58 = pred[512,2,2048]{2,1,0:T(4,128)(4,1)} reshape(pred[1024,2048]{1,0:T(8,128)(4,1)S(1)} %iota_compare_fusion.1) | data formatting | bytes 4194304 | tf_op jit(solution)/shard_map/eq | solution.py:33
  170.7 17.9 %all-to-all-done.3 = bf16[4,192,1024]{2,1,0:T(8,128)(2,1)} async-done(((bf16[4,192,1024]{2,1,0:T(8,128)(2,1)}), bf16[4,192,1024]{2,1,0:T(8,128)(2,1)}, u32[]{:S(2)}, u32[]{:S(2)}) %all-to-all-start.3) | async-done | bytes 1572896 | tf_op jit(solution)/shard_map/all_to_all | solution.py:84
  188.6 6.4 %all-to-all-start.1 = ((bf16[192,2,32,32]{0,3,1,2:T(8,128)(2,1)}), bf16[192,2,32,32]{0,3,1,2:T(8,128)(2,1)S(1)}, u32[]{:S(2)}, u32[]{:S(2)}) async-start(bf16[192,2,32,32]{0,3,1,2:T(8,128)(2,1)} %copy.64), calls=%async_computation.3 | async-start | bytes 2097152 | tf_op jit(solution)/shard_map/all_to_all | solution.py:93
  195.0 7.0 %convolution_convert_fusion.2 = bf16[2,768,768]{2,1,0:T(8,128)(2,1)} fusion(bf16[2,1024,768]{2,1,0:T(8,128)(2,1)} %bitcast.62, bf16[2,1024,768]{2,1,0:T(8,128)(2,1)} %copy-done.12), kind=kOutput, calls=%fused_computation.27 | convolution fusion | flops 2417098752 | bytes 8650752 | tf_op jit(solution)/shard_map/xsd,xsf->xdf/dot_general | solution.py:104
  206.4 5.5 %all-to-all-done.1 = bf16[192,2,32,32]{0,3,1,2:T(8,128)(2,1)S(1)} async-done(((bf16[192,2,32,32]{0,3,1,2:T(8,128)(2,1)}), bf16[192,2,32,32]{0,3,1,2:T(8,128)(2,1)S(1)}, u32[]{:S(2)}, u32[]{:S(2)}) %all-to-all-start.1) | async-done | bytes 786464 | tf_op jit(solution)/shard_map/all_to_all | solution.py:93
  211.9 4.0 %all-to-all-start.4 = ((bf16[192,2,32,32]{0,3,1,2:T(8,128)(2,1)}), bf16[192,2,32,32]{0,3,1,2:T(8,128)(2,1)S(1)}, u32[]{:S(2)}, u32[]{:S(2)}) async-start(bf16[192,2,32,32]{0,3,1,2:T(8,128)(2,1)} %copy.72), calls=%async_computation.7 | async-start | bytes 2097152 | tf_op jit(solution)/shard_map/all_to_all | solution.py:93
  215.9 7.1 %convolution_convert_fusion.1 = bf16[2,768,768]{2,1,0:T(8,128)(2,1)} fusion(bf16[2,1024,768]{2,1,0:T(8,128)(2,1)} %copy-done.11, bf16[2,1024,768]{2,1,0:T(8,128)(2,1)} %bitcast.64), kind=kOutput, calls=%fused_computation.26 | convolution fusion | flops 2417098752 | bytes 8650752 | tf_op jit(solution)/shard_map/xsf,xsd->xfd/dot_general | solution.py:101
  223.1 4.3 %fusion.17 = bf16[512,192]{0,1:T(8,128)(2,1)} fusion(bf16[192,2048,1]{0,1,2:T(8,128)(2,1)S(1)} %bitcast.72, pred[512,2,2048]{2,1,0:T(4,128)(4,1)S(1)} %copy-done, f32[512,2]{0,1:T(2,128)S(1)} %copy-done.6), kind=kOutput, calls=%fused_computation.33 | convolution fusion | flops 805601280 | bytes 3084288 | tf_op jit(solution)/shard_map/dot_general | solution.py:119
  227.4 5.4 %all-to-all-done.4 = bf16[192,2,32,32]{0,3,1,2:T(8,128)(2,1)S(1)} async-done(((bf16[192,2,32,32]{0,3,1,2:T(8,128)(2,1)}), bf16[192,2,32,32]{0,3,1,2:T(8,128)(2,1)S(1)}, u32[]{:S(2)}, u32[]{:S(2)}) %all-to-all-start.4) | async-done | bytes 786464 | tf_op jit(solution)/shard_map/all_to_all | solution.py:93
  232.8 6.4 %fusion.20 = bf16[512,192]{0,1:T(8,128)(2,1)} fusion(bf16[192,2048,1]{0,1,2:T(8,128)(2,1)S(1)} %bitcast.71, pred[512,2,2048]{2,1,0:T(4,128)(4,1)} %eq.58), kind=kOutput, calls=%fused_computation.34 | convolution fusion | flops 805404672 | bytes 3080192 | tf_op jit(solution)/shard_map/dot_general | solution.py:119
  (65 shorter events, 31.2 us)
Async XLA Ops:
  7.2 3.4 %copy-start.4 = (bf16[512,192]{0,1:T(8,128)(2,1)S(1)}, bf16[512,192]{0,1:T(8,128)(2,1)}, u32[]{:S(2)}) copy-start(bf16[512,192]{0,1:T(8,128)(2,1)} %param.6) | copy-start | bytes 589828
  27.4 10.6 %copy-start.6 = (f32[512,2]{0,1:T(2,128)S(1)}, f32[512,2]{0,1:T(2,128)}, u32[]{:S(2)}) copy-start(f32[512,2]{0,1:T(2,128)} %param.8) | copy-start | bytes 12292
  27.4 50.2 %all-to-all-start = ((bf16[2,32,32,768]{3,2,0,1:T(8,128)(2,1)}), bf16[2,32,32,768]{3,2,0,1:T(8,128)(2,1)S(1)}, u32[]{:S(2)}, u32[]{:S(2)}) async-start(bf16[2,32,32,768]{3,2,0,1:T(8,128)(2,1)} %copy.59), calls=%async_computation | async-start | bytes 6291456 | tf_op jit(solution)/shard_map/all_to_all | solution.py:51
  37.9 129.1 %reduce-scatter.6.cloned.1.call-start = ((), (), s32[]{:S(2)}) async-start(), calls=%async_computation.9 | async-start | bytes 1966080 | tf_op jit(solution)/shard_map/reduce_scatter | solution.py:81
  38.3 3.8 %copy-start.5 = (bf16[512,192]{0,1:T(8,128)(2,1)S(1)}, bf16[512,192]{0,1:T(8,128)(2,1)}, u32[]{:S(2)}) copy-start(bf16[512,192]{0,1:T(8,128)(2,1)} %param.7) | copy-start | bytes 589828
  77.7 2.8 %copy-start.9 = (bf16[2,768,768]{2,1,0:T(8,128)(2,1)S(1)}, bf16[2,768,768]{2,1,0:T(8,128)(2,1)}, u32[]{:S(2)}) copy-start(bf16[2,768,768]{2,1,0:T(8,128)(2,1)} %param.10) | copy-start | bytes 7077892
  77.9 7.5 %copy-start.1 = (bf16[2,32,32,768]{3,2,1,0:T(8,128)(2,1)}, bf16[2,32,32,768]{3,2,1,0:T(8,128)(2,1)S(1)}, u32[]{:S(2)}) copy-start(bf16[2,32,32,768]{3,2,1,0:T(8,128)(2,1)S(1)} %copy.60) | copy-start | bytes 9437188
  80.4 6.7 %copy-start.7 = (bf16[2,768,768]{2,1,0:T(8,128)(2,1)S(1)}, bf16[2,768,768]{2,1,0:T(8,128)(2,1)}, u32[]{:S(2)}) copy-start(bf16[2,768,768]{2,1,0:T(8,128)(2,1)} %param.11) | copy-start | bytes 7077892
  85.4 1.6 copy-start.11
  87.1 2.6 %copy-start.3 = (bf16[2048,768]{1,0:T(8,128)(2,1)S(1)}, bf16[2048,768]{1,0:T(8,128)(2,1)}, u32[]{:S(2)}) copy-start(bf16[2048,768]{1,0:T(8,128)(2,1)} %multiply_convert_fusion.2) | copy-start | bytes 9437188
  91.7 44.2 %all-to-all-start.2 = ((bf16[2,32,32,768]{3,2,0,1:T(8,128)(2,1)}), bf16[2,32,32,768]{3,2,0,1:T(8,128)(2,1)S(1)}, u32[]{:S(2)}, u32[]{:S(2)}) async-start(bf16[2,32,32,768]{3,2,0,1:T(8,128)(2,1)} %copy.68), calls=%async_computation.4 | async-start | bytes 6291456 | tf_op jit(solution)/shard_map/all_to_all | solution.py:51
  96.1 72.1 %reduce-scatter.4.cloned.1.call-start = ((), (), s32[]{:S(2)}) async-start(), calls=%async_computation.8 | async-start | bytes 1966080 | tf_op jit(solution)/shard_map/reduce_scatter | solution.py:81
  100.8 103.2 %reduce-scatter.8.cloned.1.call-start = ((), (), s32[]{:S(2)}) async-start(), calls=%async_computation.10 | async-start | bytes 1966080 | tf_op jit(solution)/shard_map/reduce_scatter | solution.py:81
  135.9 2.8 %copy-start.8 = (bf16[2,768,768]{2,1,0:T(8,128)(2,1)S(1)}, bf16[2,768,768]{2,1,0:T(8,128)(2,1)}, u32[]{:S(2)}) copy-start(bf16[2,768,768]{2,1,0:T(8,128)(2,1)} %param.11) | copy-start | bytes 7077892
  136.2 8.5 %copy-start.2 = (bf16[2,32,32,768]{3,2,1,0:T(8,128)(2,1)}, bf16[2,32,32,768]{3,2,1,0:T(8,128)(2,1)S(1)}, u32[]{:S(2)}) copy-start(bf16[2,32,32,768]{3,2,1,0:T(8,128)(2,1)S(1)} %copy.69) | copy-start | bytes 9437188
  138.8 7.6 %copy-start.10 = (bf16[2,768,768]{2,1,0:T(8,128)(2,1)S(1)}, bf16[2,768,768]{2,1,0:T(8,128)(2,1)}, u32[]{:S(2)}) copy-start(bf16[2,768,768]{2,1,0:T(8,128)(2,1)} %param.10) | copy-start | bytes 7077892
  144.7 1.7 copy-start.12
  152.9 35.7 %all-to-all-start.3 = ((bf16[4,192,1024]{2,1,0:T(8,128)(2,1)}), bf16[4,192,1024]{2,1,0:T(8,128)(2,1)}, u32[]{:S(2)}, u32[]{:S(2)}) async-start(bf16[4,192,1024]{2,1,0:T(8,128)(2,1)} %bitcast.22), calls=%async_computation.6 | async-start | bytes 3145728 | tf_op jit(solution)/shard_map/all_to_all | solution.py:84
  188.6 23.3 %all-to-all-start.1 = ((bf16[192,2,32,32]{0,3,1,2:T(8,128)(2,1)}), bf16[192,2,32,32]{0,3,1,2:T(8,128)(2,1)S(1)}, u32[]{:S(2)}, u32[]{:S(2)}) async-start(bf16[192,2,32,32]{0,3,1,2:T(8,128)(2,1)} %copy.64), calls=%async_computation.3 | async-start | bytes 2097152 | tf_op jit(solution)/shard_map/all_to_all | solution.py:93
  211.9 20.8 %all-to-all-start.4 = ((bf16[192,2,32,32]{0,3,1,2:T(8,128)(2,1)}), bf16[192,2,32,32]{0,3,1,2:T(8,128)(2,1)S(1)}, u32[]{:S(2)}, u32[]{:S(2)}) async-start(bf16[192,2,32,32]{0,3,1,2:T(8,128)(2,1)} %copy.72), calls=%async_computation.7 | async-start | bytes 2097152 | tf_op jit(solution)/shard_map/all_to_all | solution.py:93
  215.9 7.2 %copy-start = (pred[512,2,2048]{2,1,0:T(4,128)(4,1)S(1)}, pred[512,2,2048]{2,1,0:T(4,128)(4,1)}, u32[]{:S(2)}) copy-start(pred[512,2,2048]{2,1,0:T(4,128)(4,1)} %eq.58) | copy-start | bytes 6291460
Sparse Core Ops, SparseCore 0:
  89.8 22.9 reduce-scatter.5
  115.8 25.3 reduce-scatter.3
  149.0 32.6 reduce-scatter.7

commit v6 on v4

--- a/solution.py
+++ b/solution.py
@@ -108,9 +108,7 @@
     in_home = send_home(in_part)
 
     def gather_back(returned):
-        picked = lax.dot_general(
-            placer, returned, (((0,), (1,)), ((), ())), preferred_element_type=jnp.float32
-        )
+        picked = jnp.take(returned.T, target, axis=0).astype(jnp.float32)
         return picked.reshape(tok_rows, 2, returned.shape[0])
 
     layer_out = jnp.sum(gates[:, :, None] * gather_back(out_home), axis=1).astype(jnp.bfloat16)

time: 241 us -> 246 us (1.021)
  matrix products: 59.6 us -> 46 us
  waiting for transfers between devices: 80.2 us -> 92.7 us
  local copies, waits for them, and re-layouts: 29.7 us -> 33.2 us
  other arithmetic: 3.13 us -> 5.99 us
    reduce_scatter x4, waiting for transfers between devices: 20.6 us -> 37.9 us  [send_home(): lax.psum_scatter(part, 'ffn', scatter_dimension=0, tiled=True)]
    dot_general x2 -> x0, matrix products: 10.7 us -> none  [gather_back(): lax.dot_general(placer, returned, (((0,), (1,)), ((), ())), preferred_ele...]
    gather x0 -> x2, local copies, waits for them, and re-layouts: none -> 8.91 us  [gather_back(): picked = jnp.take(returned.T, target, axis=0).astype(jnp.float32)]
    eq x1, local copies, waits for them, and re-layouts: 7.81 us -> 0.17 us  [slot_targets(): onehot = (flat_ids[:, None] == columns).astype(jnp.bfloat16)]
    all_to_all x2, waiting for transfers between devices: 5.43 us -> 0.66 us  [send_home(): lax.all_to_all(cols, 'expert', split_axis=2, concat_axis=2, tiled=True)]
    reduce_sum x0 -> x2, other arithmetic: none -> 4.34 us  [the longest x1 2.87 us: shards(): jnp.sum(gates[:, :, None] * gather_back(out_home), axis=1)]
    dot_general x1, matrix products: 7.01 us -> 4.07 us  [shards(): jnp.einsum('xsd,xsf->xdf', rows_in, pre_grad, preferred_element_type=jnp....]
    unnamed x28 -> x34, local copies, waits for them, and re-layouts: 9.39 us -> 11 us
  transfers between devices with their start and end apart: 8 -> 8, of which waited for: 4 -> 5; matrix products, arithmetic and copies ran while one was open for 26% -> 21% of each run, Pallas kernels for 0% -> 0%
where the time goes in v6:
time: 246 us
  waiting for transfers between devices  92.7 us (38%)
  matrix products  46 us (19%)
  local copies, waits for them, and re-layouts  33.2 us (13%)
  starting transfers between devices  28 us (11%)
  blocking collectives  25.6 us (10%)
  between operations  14.1 us (6%)
  other arithmetic  5.99 us (2%)
    all_to_all x2, waiting for transfers between devices, dispatch(): lax.all_to_all(send, 'expert', split_axis=1, concat_axis=1, tiled=True)  54.1 us
    reduce_scatter x4, waiting for transfers between devices, send_home(): lax.psum_scatter(part, 'ffn', scatter_dimension=0, tiled=True)  37.9 us
    all_to_all x2, starting transfers between devices, dispatch(): lax.all_to_all(send, 'expert', split_axis=1, concat_axis=1, tiled=True)  14.9 us
    all_to_all x2, starting transfers between devices, send_home(): lax.all_to_all(cols, 'expert', split_axis=2, concat_axis=2, tiled=True)  12.9 us
    all_gather x1, blocking collectives, shards(): whole_tokens = lax.all_gather(tokens, 'ffn', axis=1, tiled=True)  12.9 us
    all_gather x1, blocking collectives, shards(): whole_cot = lax.all_gather(cotangent, 'ffn', axis=1, tiled=True)  12.8 us
    unnamed x34, local copies, waits for them, and re-layouts  11 us
    gather x2, local copies, waits for them, and re-layouts, gather_back(): picked = jnp.take(returned.T, target, axis=0).astype(jnp.float32)  8.91 us
  transfers between devices with their start and end apart: 8, of which 5 were waited for; matrix products, arithmetic and copies ran while one was open for 21% of the time, Pallas kernels for 0%

profile of v6, /device:TPU:1, one launch (start us, length us, event | category | flops | bytes accessed | tf_op | source)
XLA Modules:
  0.0 245.7 jit_solution(17978333988940651361)
XLA Ops:
  10.5 12.9 %all_gather.6 = bf16[512,768]{0,1:T(8,128)(2,1)S(1)} all-gather(bf16[512,192]{0,1:T(8,128)(2,1)S(1)} %copy-done.5), channel_id=1, replica_groups=mesh['expert'=32,'ffn'=4] {'ffn'}, dimensions={1}, use_global_device_ids=true | all-gather | bytes 983040 | tf_op jit(solution)/shard_map/all_gather | solution.py:46
  27.4 10.5 %all-to-all-start = ((bf16[2,32,32,768]{3,2,0,1:T(8,128)(2,1)}), bf16[2,32,32,768]{3,2,0,1:T(8,128)(2,1)S(1)}, u32[]{:S(2)}, u32[]{:S(2)}) async-start(bf16[2,32,32,768]{3,2,0,1:T(8,128)(2,1)} %copy.57), calls=%async_computation | async-start | bytes 6291456 | tf_op jit(solution)/shard_map/all_to_all | solution.py:51
  38.3 3.7 %fusion = f32[1,2048]{1,0:T(1,128)S(1)} fusion(f32[1024,1]{0,1:T(1,128)S(1)} %reshape.155, s32[1024]{0:T(1024)S(1)} %get-tuple-element.16), kind=kOutput, calls=%fused_computation.3 | convolution fusion | flops 27262976 | bytes 16384 | tf_op jit(solution)/shard_map/dot_general | solution.py:39
  42.1 12.8 %all_gather.7 = bf16[512,768]{0,1:T(8,128)(2,1)S(1)} all-gather(bf16[512,192]{0,1:T(8,128)(2,1)S(1)} %copy-done.6), channel_id=1, replica_groups=mesh['expert'=32,'ffn'=4] {'ffn'}, dimensions={1}, use_global_device_ids=true | all-gather | bytes 983040 | tf_op jit(solution)/shard_map/all_gather | solution.py:47
  54.8 3.8 %multiply_convert_fusion.2 = bf16[2048,768]{1,0:T(8,128)(2,1)} fusion(bf16[512,768]{0,1:T(8,128)(2,1)S(1)} %all_gather.7, f32[2048]{0:T(1024)S(1)} %bitcast.70, s32[512]{0:T(512)S(1)} %get-tuple-element.14, s32[512]{0:T(512)S(1)} %get-tuple-element.13), kind=kOutput, calls=%fused_computation.7 | convolution fusion | flops 1616904192 | bytes 3944448 | tf_op jit(solution)/shard_map/dot_general | solution.py:60
  58.6 19.0 %all-to-all-done = bf16[2,32,32,768]{3,2,0,1:T(8,128)(2,1)S(1)} async-done(((bf16[2,32,32,768]{3,2,0,1:T(8,128)(2,1)}), bf16[2,32,32,768]{3,2,0,1:T(8,128)(2,1)S(1)}, u32[]{:S(2)}, u32[]{:S(2)}) %all-to-all-start) | async-done | bytes 3145760 | tf_op jit(solution)/shard_map/all_to_all | solution.py:51
  80.4 5.0 %multiply_convert_fusion.1 = (bf16[2,1024,768]{2,1,0:T(8,128)(2,1)S(1)}, f32[2,1024,768]{2,1,0:T(8,128)}) fusion(bf16[2,1024,768]{2,1,0:T(8,128)(2,1)S(1)} %bitcast.60, bf16[2,768,768]{2,1,0:T(8,128)(2,1)S(1)} %copy-done.10), kind=kOutput, calls=%fused_computation.5 | convolution fusion | flops 2423783424 | bytes 14942208 | tf_op jit(solution)/shard_map/xsd,xdf->xsf/dot_general | solution.py:66
  87.1 2.6 %bitcast_convert_fusion.2 = bf16[768,1024]{1,0:T(8,128)(2,1)} fusion(bf16[2,1024,768]{2,1,0:T(8,128)(2,1)S(1)} %get-tuple-element.19, bf16[2,768,768]{2,1,0:T(8,128)(2,1)S(1)} %copy-done.8), kind=kOutput, calls=%fused_computation.17 | convolution fusion | flops 1208745984 | bytes 4325376 | tf_op jit(solution)/shard_map/fd,sf->ds/dot_general | solution.py:71
  91.6 4.4 %all-to-all-start.2 = ((bf16[2,32,32,768]{3,2,0,1:T(8,128)(2,1)}), bf16[2,32,32,768]{3,2,0,1:T(8,128)(2,1)S(1)}, u32[]{:S(2)}, u32[]{:S(2)}) async-start(bf16[2,32,32,768]{3,2,0,1:T(8,128)(2,1)} %copy.64), calls=%async_computation.4 | async-start | bytes 6291456 | tf_op jit(solution)/shard_map/all_to_all | solution.py:51
  96.1 4.6 %bitcast_convert_fusion.3 = bf16[768,1024]{1,0:T(8,128)(2,1)} fusion(bf16[2,1024,768]{2,1,0:T(8,128)(2,1)} %copy-done.12, bf16[2,768,768]{2,1,0:T(8,128)(2,1)} %param.13), kind=kOutput, calls=%fused_computation.18 | convolution fusion | flops 1208745984 | bytes 4325376 | tf_op jit(solution)/shard_map/fd,sf->ds/dot_general | solution.py:71
  100.8 35.1 %all-to-all-done.2 = bf16[2,32,32,768]{3,2,0,1:T(8,128)(2,1)S(1)} async-done(((bf16[2,32,32,768]{3,2,0,1:T(8,128)(2,1)}), bf16[2,32,32,768]{3,2,0,1:T(8,128)(2,1)S(1)}, u32[]{:S(2)}, u32[]{:S(2)}) %all-to-all-start.2) | async-done | bytes 3145760 | tf_op jit(solution)/shard_map/all_to_all | solution.py:51
  136.1 2.6 %copy-done.9 = bf16[2,768,768]{2,1,0:T(8,128)(2,1)S(1)} copy-done((bf16[2,768,768]{2,1,0:T(8,128)(2,1)S(1)}, bf16[2,768,768]{2,1,0:T(8,128)(2,1)}, u32[]{:S(2)}) %copy-start.9) | copy-done | bytes 2359320
  138.7 5.9 %multiply_convert_fusion = bf16[2,1024,768]{2,1,0:T(8,128)(2,1)S(1)} fusion(f32[2,1024,768]{2,1,0:T(8,128)} %get-tuple-element.20, bf16[2,1024,768]{2,1,0:T(8,128)(2,1)S(1)} %bitcast.62, bf16[2,768,768]{2,1,0:T(8,128)(2,1)S(1)} %copy-done.9), kind=kOutput, calls=%fused_computation.4 | convolution fusion | flops 2430074880 | bytes 14942208 | tf_op jit(solution)/shard_map/xsd,xfd->xsf/dot_general | solution.py:89
  146.2 2.6 %bitcast_convert_fusion = bf16[768,1024]{1,0:T(8,128)(2,1)} fusion(bf16[2,1024,768]{2,1,0:T(8,128)(2,1)S(1)} %multiply_convert_fusion, bf16[2,768,768]{2,1,0:T(8,128)(2,1)S(1)} %copy-done.11), kind=kOutput, calls=%fused_computation.15 | convolution fusion | flops 1208745984 | bytes 4325376 | tf_op jit(solution)/shard_map/df,sf->ds/dot_general | solution.py:101
  148.8 4.0 %bitcast_convert_fusion.1 = bf16[768,1024]{1,0:T(8,128)(2,1)} fusion(bf16[2,1024,768]{2,1,0:T(8,128)(2,1)} %copy-done.13, bf16[2,768,768]{2,1,0:T(8,128)(2,1)S(1)} %copy-done.11), kind=kOutput, calls=%fused_computation.16 | convolution fusion | flops 1208745984 | bytes 4325376 | tf_op jit(solution)/shard_map/df,sf->ds/dot_general | solution.py:101
  156.6 4.5 %all-to-all-start.1 = ((bf16[192,2,32,32]{0,3,1,2:T(8,128)(2,1)}), bf16[192,2,32,32]{0,3,1,2:T(8,128)(2,1)S(1)}, u32[]{:S(2)}, u32[]{:S(2)}) async-start(bf16[192,2,32,32]{0,3,1,2:T(8,128)(2,1)} %copy.62), calls=%async_computation.3 | async-start | bytes 2097152 | tf_op jit(solution)/shard_map/all_to_all | solution.py:85
  161.1 10.7 %reduce-scatter.11.cloned.1.call-done = bf16[192,1024]{1,0:T(8,128)(2,1)} async-done(((bf16[768,1024]{1,0:T(8,128)(2,1)}), bf16[192,1024]{1,0:T(8,128)(2,1)}) %reduce-scatter.11.cloned.1.call-update) | async-done | bytes 393232 | tf_op jit(solution)/shard_map/reduce_scatter | solution.py:81
  173.0 27.1 %reduce-scatter.9.cloned.1.call-done = bf16[192,1024]{1,0:T(8,128)(2,1)} async-done(((bf16[768,1024]{1,0:T(8,128)(2,1)}), bf16[192,1024]{1,0:T(8,128)(2,1)}) %reduce-scatter.9.cloned.1.call-update) | async-done | bytes 393232 | tf_op jit(solution)/shard_map/reduce_scatter | solution.py:81
  202.6 8.4 %all-to-all-start.3 = ((bf16[192,2,32,32]{0,3,1,2:T(8,128)(2,1)}), bf16[192,2,32,32]{0,3,1,2:T(8,128)(2,1)S(1)}, u32[]{:S(2)}, u32[]{:S(2)}) async-start(bf16[192,2,32,32]{0,3,1,2:T(8,128)(2,1)} %copy.68), calls=%async_computation.7 | async-start | bytes 2097152 | tf_op jit(solution)/shard_map/all_to_all | solution.py:85
  211.1 7.1 %convolution_convert_fusion.1 = bf16[2,768,768]{2,1,0:T(8,128)(2,1)} fusion(bf16[2,1024,768]{2,1,0:T(8,128)(2,1)} %copy-done.12, bf16[2,1024,768]{2,1,0:T(8,128)(2,1)} %bitcast.63), kind=kOutput, calls=%fused_computation.23 | convolution fusion | flops 2417098752 | bytes 8650752 | tf_op jit(solution)/shard_map/xsf,xsd->xfd/dot_general | solution.py:93
  218.2 4.1 %convolution_convert_fusion.2 = bf16[2,768,768]{2,1,0:T(8,128)(2,1)} fusion(bf16[2,1024,768]{2,1,0:T(8,128)(2,1)S(1)} %bitcast.61, bf16[2,1024,768]{2,1,0:T(8,128)(2,1)S(1)} %copy-done.14), kind=kOutput, calls=%fused_computation.24 | convolution fusion | flops 2417098752 | bytes 8650752 | tf_op jit(solution)/shard_map/xsd,xsf->xdf/dot_general | solution.py:96
  222.4 5.0 %gather_fusion = bf16[1024,192]{1,0:T(8,128)(2,1)} fusion(bf16[2048,192]{1,0:T(8,128)(2,1)S(1)} %bitcast.59, s32[1024]{0:T(1024)S(1)} %fusion.38), kind=kCustom, calls=%fused_computation.clone | custom fusion | bytes 790528 | tf_op jit(solution)/shard_map/jit(_take)/gather | solution.py:111
  228.1 3.9 %gather_fusion.1 = bf16[1024,192]{1,0:T(8,128)(2,1)S(1)} fusion(bf16[2048,192]{1,0:T(8,128)(2,1)S(1)} %bitcast.58, s32[1024]{0:T(1024)S(1)} %fusion.38), kind=kCustom, calls=%fused_computation.1.clone | custom fusion | bytes 790528 | tf_op jit(solution)/shard_map/jit(_take)/gather | solution.py:111
  235.4 2.9 %multiply_reduce_fusion = bf16[512,192]{1,0:T(8,128)(2,1)S(1)} fusion(f32[512,2,192]{2,1,0:T(2,128)S(1)} %reshape.132, f32[512,2]{1,0:T(8,128)S(1)} %copy.48), kind=kLoop, calls=%fused_computation.41 | loop fusion | flops 294912 | bytes 987136 | tf_op jit(solution)/shard_map/reduce_sum | solution.py:114
  (75 shorter events, 28.5 us)
Async XLA Ops:
  7.2 3.4 %copy-start.5 = (bf16[512,192]{0,1:T(8,128)(2,1)S(1)}, bf16[512,192]{0,1:T(8,128)(2,1)}, u32[]{:S(2)}) copy-start(bf16[512,192]{0,1:T(8,128)(2,1)} %param.8) | copy-start | bytes 589828
  27.4 10.6 %copy-start.7 = (f32[512,2]{0,1:T(2,128)S(1)}, f32[512,2]{0,1:T(2,128)}, u32[]{:S(2)}) copy-start(f32[512,2]{0,1:T(2,128)} %param.10) | copy-start | bytes 12292
  27.4 50.2 %all-to-all-start = ((bf16[2,32,32,768]{3,2,0,1:T(8,128)(2,1)}), bf16[2,32,32,768]{3,2,0,1:T(8,128)(2,1)S(1)}, u32[]{:S(2)}, u32[]{:S(2)}) async-start(bf16[2,32,32,768]{3,2,0,1:T(8,128)(2,1)} %copy.57), calls=%async_computation | async-start | bytes 6291456 | tf_op jit(solution)/shard_map/all_to_all | solution.py:51
  37.9 114.9 %reduce-scatter.7.cloned.1.call-start = ((), (), s32[]{:S(2)}) async-start(), calls=%async_computation.9 | async-start | bytes 1966080 | tf_op jit(solution)/shard_map/reduce_scatter | solution.py:81
  38.3 3.8 %copy-start.6 = (bf16[512,192]{0,1:T(8,128)(2,1)S(1)}, bf16[512,192]{0,1:T(8,128)(2,1)}, u32[]{:S(2)}) copy-start(bf16[512,192]{0,1:T(8,128)(2,1)} %param.9) | copy-start | bytes 589828
  77.6 2.8 %copy-start.10 = (bf16[2,768,768]{2,1,0:T(8,128)(2,1)S(1)}, bf16[2,768,768]{2,1,0:T(8,128)(2,1)}, u32[]{:S(2)}) copy-start(bf16[2,768,768]{2,1,0:T(8,128)(2,1)} %param.12) | copy-start | bytes 7077892
  77.9 7.5 %copy-start = (bf16[2,32,32,768]{3,2,1,0:T(8,128)(2,1)}, bf16[2,32,32,768]{3,2,1,0:T(8,128)(2,1)S(1)}, u32[]{:S(2)}) copy-start(bf16[2,32,32,768]{3,2,1,0:T(8,128)(2,1)S(1)} %copy.58) | copy-start | bytes 9437188
  80.4 6.6 %copy-start.8 = (bf16[2,768,768]{2,1,0:T(8,128)(2,1)S(1)}, bf16[2,768,768]{2,1,0:T(8,128)(2,1)}, u32[]{:S(2)}) copy-start(bf16[2,768,768]{2,1,0:T(8,128)(2,1)} %param.13) | copy-start | bytes 7077892
  85.4 1.6 copy-start.12
  87.1 2.6 %copy-start.3 = (bf16[2048,768]{1,0:T(8,128)(2,1)S(1)}, bf16[2048,768]{1,0:T(8,128)(2,1)}, u32[]{:S(2)}) copy-start(bf16[2048,768]{1,0:T(8,128)(2,1)} %multiply_convert_fusion.2) | copy-start | bytes 9437188
  91.6 44.2 %all-to-all-start.2 = ((bf16[2,32,32,768]{3,2,0,1:T(8,128)(2,1)}), bf16[2,32,32,768]{3,2,0,1:T(8,128)(2,1)S(1)}, u32[]{:S(2)}, u32[]{:S(2)}) async-start(bf16[2,32,32,768]{3,2,0,1:T(8,128)(2,1)} %copy.64), calls=%async_computation.4 | async-start | bytes 6291456 | tf_op jit(solution)/shard_map/all_to_all | solution.py:51
  96.0 58.1 %reduce-scatter.5.cloned.1.call-start = ((), (), s32[]{:S(2)}) async-start(), calls=%async_computation.8 | async-start | bytes 1966080 | tf_op jit(solution)/shard_map/reduce_scatter | solution.py:81
  100.7 71.1 %reduce-scatter.11.cloned.1.call-start = ((), (), s32[]{:S(2)}) async-start(), calls=%async_computation.11 | async-start | bytes 1966080 | tf_op jit(solution)/shard_map/reduce_scatter | solution.py:81
  135.8 2.8 %copy-start.9 = (bf16[2,768,768]{2,1,0:T(8,128)(2,1)S(1)}, bf16[2,768,768]{2,1,0:T(8,128)(2,1)}, u32[]{:S(2)}) copy-start(bf16[2,768,768]{2,1,0:T(8,128)(2,1)} %param.13) | copy-start | bytes 7077892
  136.1 8.5 %copy-start.2 = (bf16[2,32,32,768]{3,2,1,0:T(8,128)(2,1)}, bf16[2,32,32,768]{3,2,1,0:T(8,128)(2,1)S(1)}, u32[]{:S(2)}) copy-start(bf16[2,32,32,768]{3,2,1,0:T(8,128)(2,1)S(1)} %copy.65) | copy-start | bytes 9437188
  138.7 7.5 %copy-start.11 = (bf16[2,768,768]{2,1,0:T(8,128)(2,1)S(1)}, bf16[2,768,768]{2,1,0:T(8,128)(2,1)}, u32[]{:S(2)}) copy-start(bf16[2,768,768]{2,1,0:T(8,128)(2,1)} %param.12) | copy-start | bytes 7077892
  144.6 1.6 copy-start.13
  148.8 51.4 %reduce-scatter.9.cloned.1.call-start = ((), (), s32[]{:S(2)}) async-start(), calls=%async_computation.10 | async-start | bytes 1966080 | tf_op jit(solution)/shard_map/reduce_scatter | solution.py:81
  156.6 46.1 %all-to-all-start.1 = ((bf16[192,2,32,32]{0,3,1,2:T(8,128)(2,1)}), bf16[192,2,32,32]{0,3,1,2:T(8,128)(2,1)S(1)}, u32[]{:S(2)}, u32[]{:S(2)}) async-start(bf16[192,2,32,32]{0,3,1,2:T(8,128)(2,1)} %copy.62), calls=%async_computation.3 | async-start | bytes 2097152 | tf_op jit(solution)/shard_map/all_to_all | solution.py:85
  202.6 25.4 %all-to-all-start.3 = ((bf16[192,2,32,32]{0,3,1,2:T(8,128)(2,1)}), bf16[192,2,32,32]{0,3,1,2:T(8,128)(2,1)S(1)}, u32[]{:S(2)}, u32[]{:S(2)}) async-start(bf16[192,2,32,32]{0,3,1,2:T(8,128)(2,1)} %copy.68), calls=%async_computation.7 | async-start | bytes 2097152 | tf_op jit(solution)/shard_map/all_to_all | solution.py:85
  211.1 7.1 %copy-start.1 = (bf16[2,32,32,768]{3,2,1,0:T(8,128)(2,1)S(1)}, bf16[2,32,32,768]{3,2,1,0:T(8,128)(2,1)}, u32[]{:S(2)}) copy-start(bf16[2,32,32,768]{3,2,1,0:T(8,128)(2,1)} %copy-done) | copy-start | bytes 9437188
  211.1 7.1 %copy-start.14 = (bf16[2,1024,768]{2,1,0:T(8,128)(2,1)S(1)}, bf16[2,1024,768]{2,1,0:T(8,128)(2,1)}, u32[]{:S(2)}) copy-start(bf16[2,1024,768]{2,1,0:T(8,128)(2,1)} %copy-done.13) | copy-start | bytes 9437188
  227.3 4.7 %copy-start.4 = (bf16[1024,192]{1,0:T(8,128)(2,1)S(1)}, bf16[1024,192]{1,0:T(8,128)(2,1)}, u32[]{:S(2)}) copy-start(bf16[1024,192]{1,0:T(8,128)(2,1)} %gather_fusion) | copy-start | bytes 1179652
Sparse Core Ops, SparseCore 0:
  89.8 22.9 reduce-scatter.6
  115.2 25.3 reduce-scatter.4
  148.9 22.8 reduce-scatter.10
  174.6 25.4 reduce-scatter.8
